TPU v7x, 32 devices: a whole 2x2x4 slice. The times are simulated.
32 devices in a mesh: section: 4 (over x, core), expert: 8 (over z, y).
Axes of the slice: x: 2, y: 2, z: 4, core: 2. Of those that a mesh axis runs over, the one named last changes fastest.
Arguments:
- layer_inputs: bfloat16 [4, 8, 128, 2048], P('section', None, 'expert'), may hold values from -6 to 6
- top_grad: bfloat16 [8, 128, 2048], P('section', 'expert'), may hold values from -6 to 6
- expert_ids: int32 [4, 8, 128, 4], P('section', None, 'expert'), may hold values from 0 to 7, all different within a row; in each aligned block of 16 rows (0 to 15, 16 to 31, ..., all dimensions but the last counted through in order) at most 9 rows name the same one
- router: bfloat16 [4, 2048, 8], P('section'), may hold values from -0.125 to 0.125
- norm_gain: bfloat16 [4, 2048], P('section'), may hold values from 0.099609375 to 1.8984375
- w_gate: bfloat16 [4, 8, 2048, 1024], P('section', 'expert'), may hold values from -0.125 to 0.125
- w_up: bfloat16 [4, 8, 2048, 1024], P('section', 'expert'), may hold values from -0.125 to 0.125
- w_down: bfloat16 [4, 8, 1024, 2048], P('section', 'expert'), may hold values from -0.1875 to 0.1875
Outputs:
- input_grads: bfloat16 [4, 8, 128, 2048], P('section', None, 'expert')
Inputs may be any that keep to these rules, and one draw needn't show every extreme that they name: `expert_ids`: each token names 4 different experts. Among the 16 tokens of one device in one micro-batch of one layer, no expert is named by more than 9 of them, and in some of these blocks one expert is named by exactly 9.
All inputs are finite; a program needn't handle non-finite values.
Results may differ from a plain program's by a relative error of at most 0.015.
Values may be sent and summed in bfloat16 or wider, within the bound.
No kernel may reach another device: no remote copies, remote signals or barrier semaphores. Data moves between devices by JAX's collectives and lax.ppermute only.
A program may use at most 128 MiB of HBM per device.

v0:
```python
import jax
import jax.numpy as jnp
from jax import lax
from jax.sharding import PartitionSpec as P


def shifted(shard, axis, by):
    devices = lax.axis_size(axis)
    pairs = [(i, i + by) for i in range(devices) if 0 <= i + by < devices]
    return lax.ppermute(shard, axis, pairs)


def prepare(x_rows, gain):
    x_float = x_rows.astype(jnp.float32)
    inverse = lax.rsqrt(jnp.mean(x_float * x_float, axis=-1, keepdims=True) + 1e-05)
    normed = (x_float * inverse * gain).astype(jnp.bfloat16)
    return (x_float, inverse, normed)


def expert_rows(normed_rows, grad_rows, gate_w, up_w, down_w):
    gate = jnp.dot(normed_rows, gate_w, preferred_element_type=jnp.float32)
    up_rows = jnp.dot(normed_rows, up_w, preferred_element_type=jnp.float32)
    squash = jax.nn.sigmoid(gate)
    active = gate * squash
    hidden = (active * up_rows).astype(jnp.bfloat16)
    output = jnp.dot(hidden, down_w, preferred_element_type=jnp.float32)
    dprob = jnp.sum(output * grad_rows.astype(jnp.float32), axis=-1)
    dhidden = lax.dot_general(
        grad_rows, down_w, (((1,), (1,)), ((), ())), preferred_element_type=jnp.float32
    )
    dgate = (dhidden * up_rows * squash * (1.0 + gate * (1.0 - squash))).astype(jnp.bfloat16)
    dup = (dhidden * active).astype(jnp.bfloat16)
    returned = lax.dot_general(
        dgate, gate_w, (((1,), (1,)), ((), ())), preferred_element_type=jnp.float32
    )
    returned = returned + lax.dot_general(
        dup, up_w, (((1,), (1,)), ((), ())), preferred_element_type=jnp.float32
    )
    return (returned.astype(jnp.bfloat16), dprob)


def finish(x_float, inverse, normed, gain, router_layer, ids, grad_in, pair_back, pair_prob):
    logits = jnp.dot(normed, router_layer, preferred_element_type=jnp.float32)
    raised = jnp.exp(logits)
    probs = raised / jnp.sum(raised, axis=-1, keepdims=True)
    choose = (ids[..., None] == jnp.arange(router_layer.shape[1], dtype=jnp.int32)).astype(
        jnp.float32
    )
    picked = jnp.sum(probs[..., None, :] * choose, axis=-1)
    dfull = jnp.sum(pair_prob[..., None] * choose, axis=-2)
    dlogit = probs * (dfull - jnp.sum(probs * dfull, axis=-1, keepdims=True))
    router_term = jnp.dot(
        dlogit, router_layer.astype(jnp.float32).T, precision=lax.Precision.HIGHEST
    )
    dnormed = jnp.sum(picked[..., None] * pair_back, axis=-2) + router_term
    scaled = gain * dnormed
    inner = jnp.mean(x_float * scaled, axis=-1, keepdims=True)
    result = (
        grad_in.astype(jnp.float32)
        + inverse * scaled
        - x_float * inverse * inverse * inverse * inner
    )
    return result.astype(jnp.bfloat16)


def selection(ids, experts, capacity):
    pair_ids = ids.reshape(-1)
    onehot = (pair_ids[:, None] == jnp.arange(experts, dtype=jnp.int32)[None, :]).astype(jnp.int32)
    ranks = jnp.sum(onehot * (jnp.cumsum(onehot, axis=0) - 1), axis=1)
    target = pair_ids * capacity + ranks
    return (target[:, None] == jnp.arange(experts * capacity, dtype=jnp.int32)[None, :]).astype(
        jnp.bfloat16
    )


def pack_rows(select, rows, per_token):
    repeated = jnp.repeat(rows, per_token, axis=0)
    packed = lax.dot_general(
        select, repeated, (((0,), (0,)), ((), ())), preferred_element_type=jnp.float32
    )
    return packed.astype(jnp.bfloat16)


def pick_micro(values, index):
    return lax.dynamic_index_in_dim(values, index, 0, False)


def shards(layer_inputs, top_grad, expert_ids, router, norm_gain, w_gate, w_up, w_down):
    segments = lax.axis_size("section")
    experts = lax.axis_size("expert")
    segment_index = lax.axis_index("section")
    micro = layer_inputs.shape[1]
    tok_rows = layer_inputs.shape[2]
    width = layer_inputs.shape[3]
    per_token = expert_ids.shape[3]
    capacity = min(tok_rows, per_token * tok_rows // experts + max(1, tok_rows // 16))
    slots = experts * capacity
    gain = norm_gain[0].astype(jnp.float32)
    router_layer = router[0]
    gate_layer = w_gate[0, 0]
    up_layer = w_up[0, 0]
    down_layer = w_down[0, 0]
    ids_layer = expert_ids[0]
    x_layer = layer_inputs[0]
    top_full = lax.all_gather(top_grad, "section", axis=0, tiled=True)

    def advance(step, carry):
        previous, collected = carry
        arrived = shifted(previous, "section", -1)
        position = step - (segments - 1 - segment_index)
        working = jnp.logical_and(position >= 0, position < micro)
        chosen = jnp.clip(position, 0, micro - 1)
        grad_in = jnp.where(segment_index == segments - 1, pick_micro(top_full, chosen), arrived)
        ids_now = pick_micro(ids_layer, chosen)
        select = selection(ids_now, experts, capacity)
        x_float, inverse, normed = prepare(pick_micro(x_layer, chosen), gain)
        sent_normed = pack_rows(select, normed, per_token).reshape(experts, capacity, width)
        sent_grad = pack_rows(select, grad_in, per_token).reshape(experts, capacity, width)
        got_normed, got_grad = (
            lax.all_to_all(sent_normed, "expert", split_axis=0, concat_axis=0, tiled=True),
            lax.all_to_all(sent_grad, "expert", split_axis=0, concat_axis=0, tiled=True),
        )
        rows_normed = got_normed.reshape(slots, width)
        rows_grad = got_grad.reshape(slots, width)

        def run_expert(operands):
            return expert_rows(operands[0], operands[1], gate_layer, up_layer, down_layer)

        def skip_expert(operands):
            return (jnp.zeros((slots, width), jnp.bfloat16), jnp.zeros((slots,), jnp.float32))

        returned, dprob = lax.cond(working, run_expert, skip_expert, (rows_normed, rows_grad))
        back_home, prob_home = (
            lax.all_to_all(
                returned.reshape(experts, capacity, width),
                "expert",
                split_axis=0,
                concat_axis=0,
                tiled=True,
            ),
            lax.all_to_all(
                dprob.reshape(experts, capacity).astype(jnp.bfloat16),
                "expert",
                split_axis=0,
                concat_axis=0,
                tiled=True,
            ).astype(jnp.float32),
        )
        pair_back = lax.dot_general(
            select,
            back_home.reshape(slots, width),
            (((1,), (0,)), ((), ())),
            preferred_element_type=jnp.float32,
        )
        pair_back = pair_back.reshape(tok_rows, per_token, width)
        pair_prob = jnp.dot(
            select.astype(jnp.float32), prob_home.reshape(slots), precision=lax.Precision.HIGHEST
        )
        pair_prob = pair_prob.reshape(tok_rows, per_token)
        result = finish(
            x_float, inverse, normed, gain, router_layer, ids_now, grad_in, pair_back, pair_prob
        )
        retained = pick_micro(collected, chosen)
        collected = lax.dynamic_update_index_in_dim(
            collected, jnp.where(working, result, retained), chosen, 0
        )
        return (result, collected)

    start = (
        jnp.zeros((tok_rows, width), jnp.bfloat16),
        jnp.zeros((micro, tok_rows, width), jnp.bfloat16),
    )
    final_grad, collected = lax.fori_loop(0, micro + segments - 1, advance, start)
    return collected.reshape(1, micro, tok_rows, width)


def solution(mesh):
    placed = (
        P("section", None, "expert", None),
        P("section", "expert", None),
        P("section", None, "expert", None),
        P("section", None, None),
        P("section", None),
        P("section", "expert", None, None),
        P("section", "expert", None, None),
        P("section", "expert", None, None),
    )
    return jax.shard_map(
        shards,
        mesh=mesh,
        in_specs=placed,
        out_specs=P("section", None, "expert", None),
        check_vma=False,
    )
```

profile of v0, /device:TPU:2, one launch (start us, length us, event | category | flops | bytes accessed | tf_op | source)
XLA Modules:
  0.0 932.1 jit_solution(10642153080023947241)
XLA Ops:
  2.2 7.0 all_gather.3
  9.2 922.1 %while.18 = (s32[]{:T(128)}, bf16[16,2048]{1,0:T(8,128)(2,1)S(1)}, bf16[8,16,2048]{2,1,0:T(8,128)(2,1)S(1)}, pred[]{:T(512)}, s32[]{:T(128)}, /*index=5*/bf16[8,...) while((s32[]{:T(128)}, bf16[16,2048]{1,0:T(8,128)(2,1)S(1)}, ...), condition=%wide.region_13.14_spmd.clone, body=%wide.region_0.13_spmd.clone.sunk | while | flops 1876001664 | bytes 93928576 | solution.py:173
  16.6 5.8 all-to-all-start.1
  23.9 12.8 %all-to-all-done.1 = bf16[8,9,2048]{2,1,0:T(8,128)(2,1)S(1)} async-done(((bf16[8,9,2048]{2,1,0:T(8,128)(2,1)}), bf16[8,9,2048]{2,1,0:T(8,128)(2,1)S(1)}, u32[]{:S(2)}, u32[]{:S(2)}) %all-to-all-start.1) | async-done | bytes 294944 | tf_op jit(solution)/shard_map/while/body/eval_jaxpr/all_to_all | solution.py:120
  40.5 14.4 %all-to-all-done = bf16[8,9,2048]{2,1,0:T(8,128)(2,1)S(1)} async-done(((bf16[8,9,2048]{2,1,0:T(8,128)(2,1)}), bf16[8,9,2048]{2,1,0:T(8,128)(2,1)S(1)}, u32[]{:S(2)}, u32[]{:S(2)}) %all-to-all-start) | async-done | bytes 294944 | tf_op jit(solution)/shard_map/while/body/eval_jaxpr/all_to_all | solution.py:121
  60.4 5.3 all-to-all-done.3
  69.6 9.8 %all-to-all-done.2 = bf16[8,9,2048]{2,1,0:T(8,128)(2,1)S(1)} async-done(((bf16[8,9,2048]{2,1,0:T(8,128)(2,1)}), bf16[8,9,2048]{2,1,0:T(8,128)(2,1)S(1)}, u32[]{:S(2)}, u32[]{:S(2)}) %all-to-all-start.2) | async-done | bytes 294944 | tf_op jit(solution)/shard_map/while/body/eval_jaxpr/all_to_all | solution.py:134
  82.1 4.4 collective-permute-start
  91.1 4.4 all-to-all-start.1
  97.4 8.4 all-to-all-done.1
  105.8 3.7 all-to-all-start
  109.7 10.5 %all-to-all-done = bf16[8,9,2048]{2,1,0:T(8,128)(2,1)S(1)} async-done(((bf16[8,9,2048]{2,1,0:T(8,128)(2,1)}), bf16[8,9,2048]{2,1,0:T(8,128)(2,1)S(1)}, u32[]{:S(2)}, u32[]{:S(2)}) %all-to-all-start) | async-done | bytes 294944 | tf_op jit(solution)/shard_map/while/body/eval_jaxpr/all_to_all | solution.py:121
  120.1 14.1 %conditional.3 = (bf16[72,2048]{1,0:T(8,128)(2,1)S(1)}, bf16[72]{0:T(256)(128)(2,1)S(1)}) conditional(s32[]{:T(128)} %convert_element_type.180, () %tuple.64, (bf16[8,9,2048]{2,1,0:T(8,128)(2,1)S(1)}, bf16[1024,2048]{1,0:T(8,128)(2,1)}, bf16[8,9,2048]{2,1,0:T(8,128)(2,1)S(1)}, bf16[2048,1024]{1,0:T(8,128)(2,1)}, bf16[2048,1024]{1,0:T(8,128)(2,1)}) %tuple.65), branch_computations={%region_6.6_spmd, %region_7.8_spmd} | conditional | flops 1814298624 | bytes 82280696 | solution.py:132
  134.9 5.9 all-to-all-start.3
  142.0 5.3 all-to-all-done.3
  151.3 14.9 %all-to-all-done.2 = bf16[8,9,2048]{2,1,0:T(8,128)(2,1)S(1)} async-done(((bf16[8,9,2048]{2,1,0:T(8,128)(2,1)}), bf16[8,9,2048]{2,1,0:T(8,128)(2,1)S(1)}, u32[]{:S(2)}, u32[]{:S(2)}) %all-to-all-start.2) | async-done | bytes 294944 | tf_op jit(solution)/shard_map/while/body/eval_jaxpr/all_to_all | solution.py:134
  175.3 4.1 all-to-all-start.1
  180.9 13.7 %all-to-all-done.1 = bf16[8,9,2048]{2,1,0:T(8,128)(2,1)S(1)} async-done(((bf16[8,9,2048]{2,1,0:T(8,128)(2,1)}), bf16[8,9,2048]{2,1,0:T(8,128)(2,1)S(1)}, u32[]{:S(2)}, u32[]{:S(2)}) %all-to-all-start.1) | async-done | bytes 294944 | tf_op jit(solution)/shard_map/while/body/eval_jaxpr/all_to_all | solution.py:120
  198.4 14.5 %all-to-all-done = bf16[8,9,2048]{2,1,0:T(8,128)(2,1)S(1)} async-done(((bf16[8,9,2048]{2,1,0:T(8,128)(2,1)}), bf16[8,9,2048]{2,1,0:T(8,128)(2,1)S(1)}, u32[]{:S(2)}, u32[]{:S(2)}) %all-to-all-start) | async-done | bytes 294944 | tf_op jit(solution)/shard_map/while/body/eval_jaxpr/all_to_all | solution.py:121
  212.9 14.1 %conditional.3 = (bf16[72,2048]{1,0:T(8,128)(2,1)S(1)}, bf16[72]{0:T(256)(128)(2,1)S(1)}) conditional(s32[]{:T(128)} %convert_element_type.180, () %tuple.64, (bf16[8,9,2048]{2,1,0:T(8,128)(2,1)S(1)}, bf16[1024,2048]{1,0:T(8,128)(2,1)}, bf16[8,9,2048]{2,1,0:T(8,128)(2,1)S(1)}, bf16[2048,1024]{1,0:T(8,128)(2,1)}, bf16[2048,1024]{1,0:T(8,128)(2,1)}) %tuple.65), branch_computations={%region_6.6_spmd, %region_7.8_spmd} | conditional | flops 1814298624 | bytes 82280696 | solution.py:132
  232.5 5.3 all-to-all-done.3
  241.8 13.0 %all-to-all-done.2 = bf16[8,9,2048]{2,1,0:T(8,128)(2,1)S(1)} async-done(((bf16[8,9,2048]{2,1,0:T(8,128)(2,1)}), bf16[8,9,2048]{2,1,0:T(8,128)(2,1)S(1)}, u32[]{:S(2)}, u32[]{:S(2)}) %all-to-all-start.2) | async-done | bytes 294944 | tf_op jit(solution)/shard_map/while/body/eval_jaxpr/all_to_all | solution.py:134
  263.9 3.7 all-to-all-start.1
  269.0 13.7 %all-to-all-done.1 = bf16[8,9,2048]{2,1,0:T(8,128)(2,1)S(1)} async-done(((bf16[8,9,2048]{2,1,0:T(8,128)(2,1)}), bf16[8,9,2048]{2,1,0:T(8,128)(2,1)S(1)}, u32[]{:S(2)}, u32[]{:S(2)}) %all-to-all-start.1) | async-done | bytes 294944 | tf_op jit(solution)/shard_map/while/body/eval_jaxpr/all_to_all | solution.py:120
  286.6 14.5 %all-to-all-done = bf16[8,9,2048]{2,1,0:T(8,128)(2,1)S(1)} async-done(((bf16[8,9,2048]{2,1,0:T(8,128)(2,1)}), bf16[8,9,2048]{2,1,0:T(8,128)(2,1)S(1)}, u32[]{:S(2)}, u32[]{:S(2)}) %all-to-all-start) | async-done | bytes 294944 | tf_op jit(solution)/shard_map/while/body/eval_jaxpr/all_to_all | solution.py:121
  301.1 14.1 %conditional.3 = (bf16[72,2048]{1,0:T(8,128)(2,1)S(1)}, bf16[72]{0:T(256)(128)(2,1)S(1)}) conditional(s32[]{:T(128)} %convert_element_type.180, () %tuple.64, (bf16[8,9,2048]{2,1,0:T(8,128)(2,1)S(1)}, bf16[1024,2048]{1,0:T(8,128)(2,1)}, bf16[8,9,2048]{2,1,0:T(8,128)(2,1)S(1)}, bf16[2048,1024]{1,0:T(8,128)(2,1)}, bf16[2048,1024]{1,0:T(8,128)(2,1)}) %tuple.65), branch_computations={%region_6.6_spmd, %region_7.8_spmd} | conditional | flops 1814298624 | bytes 82280696 | solution.py:132
  320.7 5.3 all-to-all-done.3
  329.9 13.0 %all-to-all-done.2 = bf16[8,9,2048]{2,1,0:T(8,128)(2,1)S(1)} async-done(((bf16[8,9,2048]{2,1,0:T(8,128)(2,1)}), bf16[8,9,2048]{2,1,0:T(8,128)(2,1)S(1)}, u32[]{:S(2)}, u32[]{:S(2)}) %all-to-all-start.2) | async-done | bytes 294944 | tf_op jit(solution)/shard_map/while/body/eval_jaxpr/all_to_all | solution.py:134
  352.1 3.7 all-to-all-start.1
  357.2 13.7 %all-to-all-done.1 = bf16[8,9,2048]{2,1,0:T(8,128)(2,1)S(1)} async-done(((bf16[8,9,2048]{2,1,0:T(8,128)(2,1)}), bf16[8,9,2048]{2,1,0:T(8,128)(2,1)S(1)}, u32[]{:S(2)}, u32[]{:S(2)}) %all-to-all-start.1) | async-done | bytes 294944 | tf_op jit(solution)/shard_map/while/body/eval_jaxpr/all_to_all | solution.py:120
  374.7 14.5 %all-to-all-done = bf16[8,9,2048]{2,1,0:T(8,128)(2,1)S(1)} async-done(((bf16[8,9,2048]{2,1,0:T(8,128)(2,1)}), bf16[8,9,2048]{2,1,0:T(8,128)(2,1)S(1)}, u32[]{:S(2)}, u32[]{:S(2)}) %all-to-all-start) | async-done | bytes 294944 | tf_op jit(solution)/shard_map/while/body/eval_jaxpr/all_to_all | solution.py:121
  389.2 14.1 %conditional.3 = (bf16[72,2048]{1,0:T(8,128)(2,1)S(1)}, bf16[72]{0:T(256)(128)(2,1)S(1)}) conditional(s32[]{:T(128)} %convert_element_type.180, () %tuple.64, (bf16[8,9,2048]{2,1,0:T(8,128)(2,1)S(1)}, bf16[1024,2048]{1,0:T(8,128)(2,1)}, bf16[8,9,2048]{2,1,0:T(8,128)(2,1)S(1)}, bf16[2048,1024]{1,0:T(8,128)(2,1)}, bf16[2048,1024]{1,0:T(8,128)(2,1)}) %tuple.65), branch_computations={%region_6.6_spmd, %region_7.8_spmd} | conditional | flops 1814298624 | bytes 82280696 | solution.py:132
  408.9 5.3 all-to-all-done.3
  418.1 13.0 %all-to-all-done.2 = bf16[8,9,2048]{2,1,0:T(8,128)(2,1)S(1)} async-done(((bf16[8,9,2048]{2,1,0:T(8,128)(2,1)}), bf16[8,9,2048]{2,1,0:T(8,128)(2,1)S(1)}, u32[]{:S(2)}, u32[]{:S(2)}) %all-to-all-start.2) | async-done | bytes 294944 | tf_op jit(solution)/shard_map/while/body/eval_jaxpr/all_to_all | solution.py:134
  440.2 3.7 all-to-all-start.1
  445.4 13.7 %all-to-all-done.1 = bf16[8,9,2048]{2,1,0:T(8,128)(2,1)S(1)} async-done(((bf16[8,9,2048]{2,1,0:T(8,128)(2,1)}), bf16[8,9,2048]{2,1,0:T(8,128)(2,1)S(1)}, u32[]{:S(2)}, u32[]{:S(2)}) %all-to-all-start.1) | async-done | bytes 294944 | tf_op jit(solution)/shard_map/while/body/eval_jaxpr/all_to_all | solution.py:120
  462.9 14.5 %all-to-all-done = bf16[8,9,2048]{2,1,0:T(8,128)(2,1)S(1)} async-done(((bf16[8,9,2048]{2,1,0:T(8,128)(2,1)}), bf16[8,9,2048]{2,1,0:T(8,128)(2,1)S(1)}, u32[]{:S(2)}, u32[]{:S(2)}) %all-to-all-start) | async-done | bytes 294944 | tf_op jit(solution)/shard_map/while/body/eval_jaxpr/all_to_all | solution.py:121
  477.4 14.1 %conditional.3 = (bf16[72,2048]{1,0:T(8,128)(2,1)S(1)}, bf16[72]{0:T(256)(128)(2,1)S(1)}) conditional(s32[]{:T(128)} %convert_element_type.180, () %tuple.64, (bf16[8,9,2048]{2,1,0:T(8,128)(2,1)S(1)}, bf16[1024,2048]{1,0:T(8,128)(2,1)}, bf16[8,9,2048]{2,1,0:T(8,128)(2,1)S(1)}, bf16[2048,1024]{1,0:T(8,128)(2,1)}, bf16[2048,1024]{1,0:T(8,128)(2,1)}) %tuple.65), branch_computations={%region_6.6_spmd, %region_7.8_spmd} | conditional | flops 1814298624 | bytes 82280696 | solution.py:132
  497.0 5.3 all-to-all-done.3
  506.2 13.0 %all-to-all-done.2 = bf16[8,9,2048]{2,1,0:T(8,128)(2,1)S(1)} async-done(((bf16[8,9,2048]{2,1,0:T(8,128)(2,1)}), bf16[8,9,2048]{2,1,0:T(8,128)(2,1)S(1)}, u32[]{:S(2)}, u32[]{:S(2)}) %all-to-all-start.2) | async-done | bytes 294944 | tf_op jit(solution)/shard_map/while/body/eval_jaxpr/all_to_all | solution.py:134
  528.4 3.7 all-to-all-start.1
  533.5 13.7 %all-to-all-done.1 = bf16[8,9,2048]{2,1,0:T(8,128)(2,1)S(1)} async-done(((bf16[8,9,2048]{2,1,0:T(8,128)(2,1)}), bf16[8,9,2048]{2,1,0:T(8,128)(2,1)S(1)}, u32[]{:S(2)}, u32[]{:S(2)}) %all-to-all-start.1) | async-done | bytes 294944 | tf_op jit(solution)/shard_map/while/body/eval_jaxpr/all_to_all | solution.py:120
  551.0 14.5 %all-to-all-done = bf16[8,9,2048]{2,1,0:T(8,128)(2,1)S(1)} async-done(((bf16[8,9,2048]{2,1,0:T(8,128)(2,1)}), bf16[8,9,2048]{2,1,0:T(8,128)(2,1)S(1)}, u32[]{:S(2)}, u32[]{:S(2)}) %all-to-all-start) | async-done | bytes 294944 | tf_op jit(solution)/shard_map/while/body/eval_jaxpr/all_to_all | solution.py:121
  565.5 14.1 %conditional.3 = (bf16[72,2048]{1,0:T(8,128)(2,1)S(1)}, bf16[72]{0:T(256)(128)(2,1)S(1)}) conditional(s32[]{:T(128)} %convert_element_type.180, () %tuple.64, (bf16[8,9,2048]{2,1,0:T(8,128)(2,1)S(1)}, bf16[1024,2048]{1,0:T(8,128)(2,1)}, bf16[8,9,2048]{2,1,0:T(8,128)(2,1)S(1)}, bf16[2048,1024]{1,0:T(8,128)(2,1)}, bf16[2048,1024]{1,0:T(8,128)(2,1)}) %tuple.65), branch_computations={%region_6.6_spmd, %region_7.8_spmd} | conditional | flops 1814298624 | bytes 82280696 | solution.py:132
  585.2 5.3 all-to-all-done.3
  594.4 13.0 %all-to-all-done.2 = bf16[8,9,2048]{2,1,0:T(8,128)(2,1)S(1)} async-done(((bf16[8,9,2048]{2,1,0:T(8,128)(2,1)}), bf16[8,9,2048]{2,1,0:T(8,128)(2,1)S(1)}, u32[]{:S(2)}, u32[]{:S(2)}) %all-to-all-start.2) | async-done | bytes 294944 | tf_op jit(solution)/shard_map/while/body/eval_jaxpr/all_to_all | solution.py:134
  621.7 13.7 %all-to-all-done.1 = bf16[8,9,2048]{2,1,0:T(8,128)(2,1)S(1)} async-done(((bf16[8,9,2048]{2,1,0:T(8,128)(2,1)}), bf16[8,9,2048]{2,1,0:T(8,128)(2,1)S(1)}, u32[]{:S(2)}, u32[]{:S(2)}) %all-to-all-start.1) | async-done | bytes 294944 | tf_op jit(solution)/shard_map/while/body/eval_jaxpr/all_to_all | solution.py:120
  639.2 14.5 %all-to-all-done = bf16[8,9,2048]{2,1,0:T(8,128)(2,1)S(1)} async-done(((bf16[8,9,2048]{2,1,0:T(8,128)(2,1)}), bf16[8,9,2048]{2,1,0:T(8,128)(2,1)S(1)}, u32[]{:S(2)}, u32[]{:S(2)}) %all-to-all-start) | async-done | bytes 294944 | tf_op jit(solution)/shard_map/while/body/eval_jaxpr/all_to_all | solution.py:121
  653.7 14.1 %conditional.3 = (bf16[72,2048]{1,0:T(8,128)(2,1)S(1)}, bf16[72]{0:T(256)(128)(2,1)S(1)}) conditional(s32[]{:T(128)} %convert_element_type.180, () %tuple.64, (bf16[8,9,2048]{2,1,0:T(8,128)(2,1)S(1)}, bf16[1024,2048]{1,0:T(8,128)(2,1)}, bf16[8,9,2048]{2,1,0:T(8,128)(2,1)S(1)}, bf16[2048,1024]{1,0:T(8,128)(2,1)}, bf16[2048,1024]{1,0:T(8,128)(2,1)}) %tuple.65), branch_computations={%region_6.6_spmd, %region_7.8_spmd} | conditional | flops 1814298624 | bytes 82280696 | solution.py:132
  673.3 5.3 all-to-all-done.3
  682.6 13.0 %all-to-all-done.2 = bf16[8,9,2048]{2,1,0:T(8,128)(2,1)S(1)} async-done(((bf16[8,9,2048]{2,1,0:T(8,128)(2,1)}), bf16[8,9,2048]{2,1,0:T(8,128)(2,1)S(1)}, u32[]{:S(2)}, u32[]{:S(2)}) %all-to-all-start.2) | async-done | bytes 294944 | tf_op jit(solution)/shard_map/while/body/eval_jaxpr/all_to_all | solution.py:134
  709.8 13.7 %all-to-all-done.1 = bf16[8,9,2048]{2,1,0:T(8,128)(2,1)S(1)} async-done(((bf16[8,9,2048]{2,1,0:T(8,128)(2,1)}), bf16[8,9,2048]{2,1,0:T(8,128)(2,1)S(1)}, u32[]{:S(2)}, u32[]{:S(2)}) %all-to-all-start.1) | async-done | bytes 294944 | tf_op jit(solution)/shard_map/while/body/eval_jaxpr/all_to_all | solution.py:120
  727.4 14.5 %all-to-all-done = bf16[8,9,2048]{2,1,0:T(8,128)(2,1)S(1)} async-done(((bf16[8,9,2048]{2,1,0:T(8,128)(2,1)}), bf16[8,9,2048]{2,1,0:T(8,128)(2,1)S(1)}, u32[]{:S(2)}, u32[]{:S(2)}) %all-to-all-start) | async-done | bytes 294944 | tf_op jit(solution)/shard_map/while/body/eval_jaxpr/all_to_all | solution.py:121
  741.9 14.1 %conditional.3 = (bf16[72,2048]{1,0:T(8,128)(2,1)S(1)}, bf16[72]{0:T(256)(128)(2,1)S(1)}) conditional(s32[]{:T(128)} %convert_element_type.180, () %tuple.64, (bf16[8,9,2048]{2,1,0:T(8,128)(2,1)S(1)}, bf16[1024,2048]{1,0:T(8,128)(2,1)}, bf16[8,9,2048]{2,1,0:T(8,128)(2,1)S(1)}, bf16[2048,1024]{1,0:T(8,128)(2,1)}, bf16[2048,1024]{1,0:T(8,128)(2,1)}) %tuple.65), branch_computations={%region_6.6_spmd, %region_7.8_spmd} | conditional | flops 1814298624 | bytes 82280696 | solution.py:132
  761.5 5.3 all-to-all-done.3
  770.7 9.8 %all-to-all-done.2 = bf16[8,9,2048]{2,1,0:T(8,128)(2,1)S(1)} async-done(((bf16[8,9,2048]{2,1,0:T(8,128)(2,1)}), bf16[8,9,2048]{2,1,0:T(8,128)(2,1)S(1)}, u32[]{:S(2)}, u32[]{:S(2)}) %all-to-all-start.2) | async-done | bytes 294944 | tf_op jit(solution)/shard_map/while/body/eval_jaxpr/all_to_all | solution.py:134
  794.8 13.7 %all-to-all-done.1 = bf16[8,9,2048]{2,1,0:T(8,128)(2,1)S(1)} async-done(((bf16[8,9,2048]{2,1,0:T(8,128)(2,1)}), bf16[8,9,2048]{2,1,0:T(8,128)(2,1)S(1)}, u32[]{:S(2)}, u32[]{:S(2)}) %all-to-all-start.1) | async-done | bytes 294944 | tf_op jit(solution)/shard_map/while/body/eval_jaxpr/all_to_all | solution.py:120
  812.3 14.5 %all-to-all-done = bf16[8,9,2048]{2,1,0:T(8,128)(2,1)S(1)} async-done(((bf16[8,9,2048]{2,1,0:T(8,128)(2,1)}), bf16[8,9,2048]{2,1,0:T(8,128)(2,1)S(1)}, u32[]{:S(2)}, u32[]{:S(2)}) %all-to-all-start) | async-done | bytes 294944 | tf_op jit(solution)/shard_map/while/body/eval_jaxpr/all_to_all | solution.py:121
  832.3 5.3 all-to-all-done.3
  841.6 13.0 %all-to-all-done.2 = bf16[8,9,2048]{2,1,0:T(8,128)(2,1)S(1)} async-done(((bf16[8,9,2048]{2,1,0:T(8,128)(2,1)}), bf16[8,9,2048]{2,1,0:T(8,128)(2,1)S(1)}, u32[]{:S(2)}, u32[]{:S(2)}) %all-to-all-start.2) | async-done | bytes 294944 | tf_op jit(solution)/shard_map/while/body/eval_jaxpr/all_to_all | solution.py:134
  868.9 13.7 %all-to-all-done.1 = bf16[8,9,2048]{2,1,0:T(8,128)(2,1)S(1)} async-done(((bf16[8,9,2048]{2,1,0:T(8,128)(2,1)}), bf16[8,9,2048]{2,1,0:T(8,128)(2,1)S(1)}, u32[]{:S(2)}, u32[]{:S(2)}) %all-to-all-start.1) | async-done | bytes 294944 | tf_op jit(solution)/shard_map/while/body/eval_jaxpr/all_to_all | solution.py:120
  886.4 14.5 %all-to-all-done = bf16[8,9,2048]{2,1,0:T(8,128)(2,1)S(1)} async-done(((bf16[8,9,2048]{2,1,0:T(8,128)(2,1)}), bf16[8,9,2048]{2,1,0:T(8,128)(2,1)S(1)}, u32[]{:S(2)}, u32[]{:S(2)}) %all-to-all-start) | async-done | bytes 294944 | tf_op jit(solution)/shard_map/while/body/eval_jaxpr/all_to_all | solution.py:121
  906.4 5.3 all-to-all-done.3
  915.6 13.0 %all-to-all-done.2 = bf16[8,9,2048]{2,1,0:T(8,128)(2,1)S(1)} async-done(((bf16[8,9,2048]{2,1,0:T(8,128)(2,1)}), bf16[8,9,2048]{2,1,0:T(8,128)(2,1)S(1)}, u32[]{:S(2)}, u32[]{:S(2)}) %all-to-all-start.2) | async-done | bytes 294944 | tf_op jit(solution)/shard_map/while/body/eval_jaxpr/all_to_all | solution.py:134
  (623 shorter events, 382.5 us)
Async XLA Ops:
  9.2 31.1 %copy-start.3 = (bf16[2048,8]{0,1:T(8,128)(2,1)S(1)}, bf16[2048,8]{0,1:T(8,128)(2,1)}, u32[]{:S(2)}) copy-start(bf16[2048,8]{0,1:T(8,128)(2,1)} %get-tuple-element.544) | copy-start | bytes 98308 | tf_op jit(solution)/shard_map/while
  9.2 13.2 %collective-permute-start = (bf16[16,2048]{1,0:T(8,128)(2,1)S(1)}, bf16[16,2048]{1,0:T(8,128)(2,1)S(1)}, u32[]{:S(2)}, u32[]{:S(2)}) collective-permute-start(bf16[16,2048]{1,0:T(8,128)(2,1)S(1)} %broadcast_select_fusion.2), channel_id=1, source_target_pairs={{8,0},{16,8},{24,16},{9,1},{17,9},{25,17},{10,2},{18,10},{26,18},{... | collective-permute-start | bytes 196616 | tf_op jit(solution)/shard_map/while/body/eval_jaxpr/ppermute | solution.py:10
  16.6 20.1 %all-to-all-start.1 = ((bf16[8,9,2048]{2,1,0:T(8,128)(2,1)}), bf16[8,9,2048]{2,1,0:T(8,128)(2,1)S(1)}, u32[]{:S(2)}, u32[]{:S(2)}) async-start(bf16[8,9,2048]{2,1,0:T(8,128)(2,1)} %reshape.265), calls=%async_computation.1 | async-start | bytes 1048576 | tf_op jit(solution)/shard_map/while/body/eval_jaxpr/all_to_all | solution.py:120
  36.7 18.2 %all-to-all-start = ((bf16[8,9,2048]{2,1,0:T(8,128)(2,1)}), bf16[8,9,2048]{2,1,0:T(8,128)(2,1)S(1)}, u32[]{:S(2)}, u32[]{:S(2)}) async-start(bf16[8,9,2048]{2,1,0:T(8,128)(2,1)} %reshape.263), calls=%async_computation | async-start | bytes 1048576 | tf_op jit(solution)/shard_map/while/body/eval_jaxpr/all_to_all | solution.py:121
  55.6 10.1 %all-to-all-start.3 = ((bf16[8,1,9]{2,1,0:T(2,128)(2,1)}), bf16[8,1,9]{2,1,0:T(2,128)(2,1)S(1)}, u32[]{:S(2)}, u32[]{:S(2)}) async-start(bf16[8,1,9]{2,1,0:T(2,128)(2,1)} %convert_element_type.181), calls=%async_computation.3 | async-start | bytes 8192 | tf_op jit(solution)/shard_map/while/body/eval_jaxpr/all_to_all | solution.py:141
  65.7 13.7 %all-to-all-start.2 = ((bf16[8,9,2048]{2,1,0:T(8,128)(2,1)}), bf16[8,9,2048]{2,1,0:T(8,128)(2,1)S(1)}, u32[]{:S(2)}, u32[]{:S(2)}) async-start(bf16[8,9,2048]{2,1,0:T(8,128)(2,1)} %reshape.266), calls=%async_computation.2 | async-start | bytes 1048576 | tf_op jit(solution)/shard_map/while/body/eval_jaxpr/all_to_all | solution.py:134
  82.1 13.8 %collective-permute-start = (bf16[16,2048]{1,0:T(8,128)(2,1)S(1)}, bf16[16,2048]{1,0:T(8,128)(2,1)S(1)}, u32[]{:S(2)}, u32[]{:S(2)}) collective-permute-start(bf16[16,2048]{1,0:T(8,128)(2,1)S(1)} %broadcast_select_fusion.2), channel_id=1, source_target_pairs={{8,0},{16,8},{24,16},{9,1},{17,9},{25,17},{10,2},{18,10},{26,18},{... | collective-permute-start | bytes 196616 | tf_op jit(solution)/shard_map/while/body/eval_jaxpr/ppermute | solution.py:10
  91.1 14.7 %all-to-all-start.1 = ((bf16[8,9,2048]{2,1,0:T(8,128)(2,1)}), bf16[8,9,2048]{2,1,0:T(8,128)(2,1)S(1)}, u32[]{:S(2)}, u32[]{:S(2)}) async-start(bf16[8,9,2048]{2,1,0:T(8,128)(2,1)} %reshape.265), calls=%async_computation.1 | async-start | bytes 1048576 | tf_op jit(solution)/shard_map/while/body/eval_jaxpr/all_to_all | solution.py:120
  105.8 14.3 %all-to-all-start = ((bf16[8,9,2048]{2,1,0:T(8,128)(2,1)}), bf16[8,9,2048]{2,1,0:T(8,128)(2,1)S(1)}, u32[]{:S(2)}, u32[]{:S(2)}) async-start(bf16[8,9,2048]{2,1,0:T(8,128)(2,1)} %reshape.263), calls=%async_computation | async-start | bytes 1048576 | tf_op jit(solution)/shard_map/while/body/eval_jaxpr/all_to_all | solution.py:121
  134.9 12.4 %all-to-all-start.3 = ((bf16[8,1,9]{2,1,0:T(2,128)(2,1)}), bf16[8,1,9]{2,1,0:T(2,128)(2,1)S(1)}, u32[]{:S(2)}, u32[]{:S(2)}) async-start(bf16[8,1,9]{2,1,0:T(2,128)(2,1)} %convert_element_type.181), calls=%async_computation.3 | async-start | bytes 8192 | tf_op jit(solution)/shard_map/while/body/eval_jaxpr/all_to_all | solution.py:141
  147.4 18.9 %all-to-all-start.2 = ((bf16[8,9,2048]{2,1,0:T(8,128)(2,1)}), bf16[8,9,2048]{2,1,0:T(8,128)(2,1)S(1)}, u32[]{:S(2)}, u32[]{:S(2)}) async-start(bf16[8,9,2048]{2,1,0:T(8,128)(2,1)} %reshape.266), calls=%async_computation.2 | async-start | bytes 1048576 | tf_op jit(solution)/shard_map/while/body/eval_jaxpr/all_to_all | solution.py:134
  168.9 29.4 %copy-start.3 = (bf16[2048,8]{0,1:T(8,128)(2,1)S(1)}, bf16[2048,8]{0,1:T(8,128)(2,1)}, u32[]{:S(2)}) copy-start(bf16[2048,8]{0,1:T(8,128)(2,1)} %get-tuple-element.544) | copy-start | bytes 98308 | tf_op jit(solution)/shard_map/while
  168.9 10.5 %collective-permute-start = (bf16[16,2048]{1,0:T(8,128)(2,1)S(1)}, bf16[16,2048]{1,0:T(8,128)(2,1)S(1)}, u32[]{:S(2)}, u32[]{:S(2)}) collective-permute-start(bf16[16,2048]{1,0:T(8,128)(2,1)S(1)} %broadcast_select_fusion.2), channel_id=1, source_target_pairs={{8,0},{16,8},{24,16},{9,1},{17,9},{25,17},{10,2},{18,10},{26,18},{... | collective-permute-start | bytes 196616 | tf_op jit(solution)/shard_map/while/body/eval_jaxpr/ppermute | solution.py:10
  175.3 19.2 %all-to-all-start.1 = ((bf16[8,9,2048]{2,1,0:T(8,128)(2,1)}), bf16[8,9,2048]{2,1,0:T(8,128)(2,1)S(1)}, u32[]{:S(2)}, u32[]{:S(2)}) async-start(bf16[8,9,2048]{2,1,0:T(8,128)(2,1)} %reshape.265), calls=%async_computation.1 | async-start | bytes 1048576 | tf_op jit(solution)/shard_map/while/body/eval_jaxpr/all_to_all | solution.py:120
  194.6 18.3 %all-to-all-start = ((bf16[8,9,2048]{2,1,0:T(8,128)(2,1)}), bf16[8,9,2048]{2,1,0:T(8,128)(2,1)S(1)}, u32[]{:S(2)}, u32[]{:S(2)}) async-start(bf16[8,9,2048]{2,1,0:T(8,128)(2,1)} %reshape.263), calls=%async_computation | async-start | bytes 1048576 | tf_op jit(solution)/shard_map/while/body/eval_jaxpr/all_to_all | solution.py:121
  227.7 10.1 %all-to-all-start.3 = ((bf16[8,1,9]{2,1,0:T(2,128)(2,1)}), bf16[8,1,9]{2,1,0:T(2,128)(2,1)S(1)}, u32[]{:S(2)}, u32[]{:S(2)}) async-start(bf16[8,1,9]{2,1,0:T(2,128)(2,1)} %convert_element_type.181), calls=%async_computation.3 | async-start | bytes 8192 | tf_op jit(solution)/shard_map/while/body/eval_jaxpr/all_to_all | solution.py:141
  237.9 16.9 %all-to-all-start.2 = ((bf16[8,9,2048]{2,1,0:T(8,128)(2,1)}), bf16[8,9,2048]{2,1,0:T(8,128)(2,1)S(1)}, u32[]{:S(2)}, u32[]{:S(2)}) async-start(bf16[8,9,2048]{2,1,0:T(8,128)(2,1)} %reshape.266), calls=%async_computation.2 | async-start | bytes 1048576 | tf_op jit(solution)/shard_map/while/body/eval_jaxpr/all_to_all | solution.py:134
  257.4 29.0 %copy-start.3 = (bf16[2048,8]{0,1:T(8,128)(2,1)S(1)}, bf16[2048,8]{0,1:T(8,128)(2,1)}, u32[]{:S(2)}) copy-start(bf16[2048,8]{0,1:T(8,128)(2,1)} %get-tuple-element.544) | copy-start | bytes 98308 | tf_op jit(solution)/shard_map/while
  257.4 10.1 %collective-permute-start = (bf16[16,2048]{1,0:T(8,128)(2,1)S(1)}, bf16[16,2048]{1,0:T(8,128)(2,1)S(1)}, u32[]{:S(2)}, u32[]{:S(2)}) collective-permute-start(bf16[16,2048]{1,0:T(8,128)(2,1)S(1)} %broadcast_select_fusion.2), channel_id=1, source_target_pairs={{8,0},{16,8},{24,16},{9,1},{17,9},{25,17},{10,2},{18,10},{26,18},{... | collective-permute-start | bytes 196616 | tf_op jit(solution)/shard_map/while/body/eval_jaxpr/ppermute | solution.py:10
  263.9 18.8 %all-to-all-start.1 = ((bf16[8,9,2048]{2,1,0:T(8,128)(2,1)}), bf16[8,9,2048]{2,1,0:T(8,128)(2,1)S(1)}, u32[]{:S(2)}, u32[]{:S(2)}) async-start(bf16[8,9,2048]{2,1,0:T(8,128)(2,1)} %reshape.265), calls=%async_computation.1 | async-start | bytes 1048576 | tf_op jit(solution)/shard_map/while/body/eval_jaxpr/all_to_all | solution.py:120
  282.8 18.3 %all-to-all-start = ((bf16[8,9,2048]{2,1,0:T(8,128)(2,1)}), bf16[8,9,2048]{2,1,0:T(8,128)(2,1)S(1)}, u32[]{:S(2)}, u32[]{:S(2)}) async-start(bf16[8,9,2048]{2,1,0:T(8,128)(2,1)} %reshape.263), calls=%async_computation | async-start | bytes 1048576 | tf_op jit(solution)/shard_map/while/body/eval_jaxpr/all_to_all | solution.py:121
  315.9 10.1 %all-to-all-start.3 = ((bf16[8,1,9]{2,1,0:T(2,128)(2,1)}), bf16[8,1,9]{2,1,0:T(2,128)(2,1)S(1)}, u32[]{:S(2)}, u32[]{:S(2)}) async-start(bf16[8,1,9]{2,1,0:T(2,128)(2,1)} %convert_element_type.181), calls=%async_computation.3 | async-start | bytes 8192 | tf_op jit(solution)/shard_map/while/body/eval_jaxpr/all_to_all | solution.py:141
  326.0 16.9 %all-to-all-start.2 = ((bf16[8,9,2048]{2,1,0:T(8,128)(2,1)}), bf16[8,9,2048]{2,1,0:T(8,128)(2,1)S(1)}, u32[]{:S(2)}, u32[]{:S(2)}) async-start(bf16[8,9,2048]{2,1,0:T(8,128)(2,1)} %reshape.266), calls=%async_computation.2 | async-start | bytes 1048576 | tf_op jit(solution)/shard_map/while/body/eval_jaxpr/all_to_all | solution.py:134
  345.6 29.0 %copy-start.3 = (bf16[2048,8]{0,1:T(8,128)(2,1)S(1)}, bf16[2048,8]{0,1:T(8,128)(2,1)}, u32[]{:S(2)}) copy-start(bf16[2048,8]{0,1:T(8,128)(2,1)} %get-tuple-element.544) | copy-start | bytes 98308 | tf_op jit(solution)/shard_map/while
  345.6 10.1 %collective-permute-start = (bf16[16,2048]{1,0:T(8,128)(2,1)S(1)}, bf16[16,2048]{1,0:T(8,128)(2,1)S(1)}, u32[]{:S(2)}, u32[]{:S(2)}) collective-permute-start(bf16[16,2048]{1,0:T(8,128)(2,1)S(1)} %broadcast_select_fusion.2), channel_id=1, source_target_pairs={{8,0},{16,8},{24,16},{9,1},{17,9},{25,17},{10,2},{18,10},{26,18},{... | collective-permute-start | bytes 196616 | tf_op jit(solution)/shard_map/while/body/eval_jaxpr/ppermute | solution.py:10
  352.1 18.8 %all-to-all-start.1 = ((bf16[8,9,2048]{2,1,0:T(8,128)(2,1)}), bf16[8,9,2048]{2,1,0:T(8,128)(2,1)S(1)}, u32[]{:S(2)}, u32[]{:S(2)}) async-start(bf16[8,9,2048]{2,1,0:T(8,128)(2,1)} %reshape.265), calls=%async_computation.1 | async-start | bytes 1048576 | tf_op jit(solution)/shard_map/while/body/eval_jaxpr/all_to_all | solution.py:120
  370.9 18.3 %all-to-all-start = ((bf16[8,9,2048]{2,1,0:T(8,128)(2,1)}), bf16[8,9,2048]{2,1,0:T(8,128)(2,1)S(1)}, u32[]{:S(2)}, u32[]{:S(2)}) async-start(bf16[8,9,2048]{2,1,0:T(8,128)(2,1)} %reshape.263), calls=%async_computation | async-start | bytes 1048576 | tf_op jit(solution)/shard_map/while/body/eval_jaxpr/all_to_all | solution.py:121
  404.0 10.1 %all-to-all-start.3 = ((bf16[8,1,9]{2,1,0:T(2,128)(2,1)}), bf16[8,1,9]{2,1,0:T(2,128)(2,1)S(1)}, u32[]{:S(2)}, u32[]{:S(2)}) async-start(bf16[8,1,9]{2,1,0:T(2,128)(2,1)} %convert_element_type.181), calls=%async_computation.3 | async-start | bytes 8192 | tf_op jit(solution)/shard_map/while/body/eval_jaxpr/all_to_all | solution.py:141
  414.2 16.9 %all-to-all-start.2 = ((bf16[8,9,2048]{2,1,0:T(8,128)(2,1)}), bf16[8,9,2048]{2,1,0:T(8,128)(2,1)S(1)}, u32[]{:S(2)}, u32[]{:S(2)}) async-start(bf16[8,9,2048]{2,1,0:T(8,128)(2,1)} %reshape.266), calls=%async_computation.2 | async-start | bytes 1048576 | tf_op jit(solution)/shard_map/while/body/eval_jaxpr/all_to_all | solution.py:134
  433.7 29.0 %copy-start.3 = (bf16[2048,8]{0,1:T(8,128)(2,1)S(1)}, bf16[2048,8]{0,1:T(8,128)(2,1)}, u32[]{:S(2)}) copy-start(bf16[2048,8]{0,1:T(8,128)(2,1)} %get-tuple-element.544) | copy-start | bytes 98308 | tf_op jit(solution)/shard_map/while
  433.8 10.1 %collective-permute-start = (bf16[16,2048]{1,0:T(8,128)(2,1)S(1)}, bf16[16,2048]{1,0:T(8,128)(2,1)S(1)}, u32[]{:S(2)}, u32[]{:S(2)}) collective-permute-start(bf16[16,2048]{1,0:T(8,128)(2,1)S(1)} %broadcast_select_fusion.2), channel_id=1, source_target_pairs={{8,0},{16,8},{24,16},{9,1},{17,9},{25,17},{10,2},{18,10},{26,18},{... | collective-permute-start | bytes 196616 | tf_op jit(solution)/shard_map/while/body/eval_jaxpr/ppermute | solution.py:10
  440.2 18.8 %all-to-all-start.1 = ((bf16[8,9,2048]{2,1,0:T(8,128)(2,1)}), bf16[8,9,2048]{2,1,0:T(8,128)(2,1)S(1)}, u32[]{:S(2)}, u32[]{:S(2)}) async-start(bf16[8,9,2048]{2,1,0:T(8,128)(2,1)} %reshape.265), calls=%async_computation.1 | async-start | bytes 1048576 | tf_op jit(solution)/shard_map/while/body/eval_jaxpr/all_to_all | solution.py:120
  459.1 18.3 %all-to-all-start = ((bf16[8,9,2048]{2,1,0:T(8,128)(2,1)}), bf16[8,9,2048]{2,1,0:T(8,128)(2,1)S(1)}, u32[]{:S(2)}, u32[]{:S(2)}) async-start(bf16[8,9,2048]{2,1,0:T(8,128)(2,1)} %reshape.263), calls=%async_computation | async-start | bytes 1048576 | tf_op jit(solution)/shard_map/while/body/eval_jaxpr/all_to_all | solution.py:121
  492.2 10.1 %all-to-all-start.3 = ((bf16[8,1,9]{2,1,0:T(2,128)(2,1)}), bf16[8,1,9]{2,1,0:T(2,128)(2,1)S(1)}, u32[]{:S(2)}, u32[]{:S(2)}) async-start(bf16[8,1,9]{2,1,0:T(2,128)(2,1)} %convert_element_type.181), calls=%async_computation.3 | async-start | bytes 8192 | tf_op jit(solution)/shard_map/while/body/eval_jaxpr/all_to_all | solution.py:141
  502.3 16.9 %all-to-all-start.2 = ((bf16[8,9,2048]{2,1,0:T(8,128)(2,1)}), bf16[8,9,2048]{2,1,0:T(8,128)(2,1)S(1)}, u32[]{:S(2)}, u32[]{:S(2)}) async-start(bf16[8,9,2048]{2,1,0:T(8,128)(2,1)} %reshape.266), calls=%async_computation.2 | async-start | bytes 1048576 | tf_op jit(solution)/shard_map/while/body/eval_jaxpr/all_to_all | solution.py:134
  521.9 29.0 %copy-start.3 = (bf16[2048,8]{0,1:T(8,128)(2,1)S(1)}, bf16[2048,8]{0,1:T(8,128)(2,1)}, u32[]{:S(2)}) copy-start(bf16[2048,8]{0,1:T(8,128)(2,1)} %get-tuple-element.544) | copy-start | bytes 98308 | tf_op jit(solution)/shard_map/while
  521.9 10.1 %collective-permute-start = (bf16[16,2048]{1,0:T(8,128)(2,1)S(1)}, bf16[16,2048]{1,0:T(8,128)(2,1)S(1)}, u32[]{:S(2)}, u32[]{:S(2)}) collective-permute-start(bf16[16,2048]{1,0:T(8,128)(2,1)S(1)} %broadcast_select_fusion.2), channel_id=1, source_target_pairs={{8,0},{16,8},{24,16},{9,1},{17,9},{25,17},{10,2},{18,10},{26,18},{... | collective-permute-start | bytes 196616 | tf_op jit(solution)/shard_map/while/body/eval_jaxpr/ppermute | solution.py:10
  528.4 18.8 %all-to-all-start.1 = ((bf16[8,9,2048]{2,1,0:T(8,128)(2,1)}), bf16[8,9,2048]{2,1,0:T(8,128)(2,1)S(1)}, u32[]{:S(2)}, u32[]{:S(2)}) async-start(bf16[8,9,2048]{2,1,0:T(8,128)(2,1)} %reshape.265), calls=%async_computation.1 | async-start | bytes 1048576 | tf_op jit(solution)/shard_map/while/body/eval_jaxpr/all_to_all | solution.py:120
  547.2 18.3 %all-to-all-start = ((bf16[8,9,2048]{2,1,0:T(8,128)(2,1)}), bf16[8,9,2048]{2,1,0:T(8,128)(2,1)S(1)}, u32[]{:S(2)}, u32[]{:S(2)}) async-start(bf16[8,9,2048]{2,1,0:T(8,128)(2,1)} %reshape.263), calls=%async_computation | async-start | bytes 1048576 | tf_op jit(solution)/shard_map/while/body/eval_jaxpr/all_to_all | solution.py:121
  580.4 10.1 %all-to-all-start.3 = ((bf16[8,1,9]{2,1,0:T(2,128)(2,1)}), bf16[8,1,9]{2,1,0:T(2,128)(2,1)S(1)}, u32[]{:S(2)}, u32[]{:S(2)}) async-start(bf16[8,1,9]{2,1,0:T(2,128)(2,1)} %convert_element_type.181), calls=%async_computation.3 | async-start | bytes 8192 | tf_op jit(solution)/shard_map/while/body/eval_jaxpr/all_to_all | solution.py:141
  590.5 16.9 %all-to-all-start.2 = ((bf16[8,9,2048]{2,1,0:T(8,128)(2,1)}), bf16[8,9,2048]{2,1,0:T(8,128)(2,1)S(1)}, u32[]{:S(2)}, u32[]{:S(2)}) async-start(bf16[8,9,2048]{2,1,0:T(8,128)(2,1)} %reshape.266), calls=%async_computation.2 | async-start | bytes 1048576 | tf_op jit(solution)/shard_map/while/body/eval_jaxpr/all_to_all | solution.py:134
  610.1 29.0 %copy-start.3 = (bf16[2048,8]{0,1:T(8,128)(2,1)S(1)}, bf16[2048,8]{0,1:T(8,128)(2,1)}, u32[]{:S(2)}) copy-start(bf16[2048,8]{0,1:T(8,128)(2,1)} %get-tuple-element.544) | copy-start | bytes 98308 | tf_op jit(solution)/shard_map/while
  610.1 10.1 %collective-permute-start = (bf16[16,2048]{1,0:T(8,128)(2,1)S(1)}, bf16[16,2048]{1,0:T(8,128)(2,1)S(1)}, u32[]{:S(2)}, u32[]{:S(2)}) collective-permute-start(bf16[16,2048]{1,0:T(8,128)(2,1)S(1)} %broadcast_select_fusion.2), channel_id=1, source_target_pairs={{8,0},{16,8},{24,16},{9,1},{17,9},{25,17},{10,2},{18,10},{26,18},{... | collective-permute-start | bytes 196616 | tf_op jit(solution)/shard_map/while/body/eval_jaxpr/ppermute | solution.py:10
  616.5 18.8 %all-to-all-start.1 = ((bf16[8,9,2048]{2,1,0:T(8,128)(2,1)}), bf16[8,9,2048]{2,1,0:T(8,128)(2,1)S(1)}, u32[]{:S(2)}, u32[]{:S(2)}) async-start(bf16[8,9,2048]{2,1,0:T(8,128)(2,1)} %reshape.265), calls=%async_computation.1 | async-start | bytes 1048576 | tf_op jit(solution)/shard_map/while/body/eval_jaxpr/all_to_all | solution.py:120
  635.4 18.3 %all-to-all-start = ((bf16[8,9,2048]{2,1,0:T(8,128)(2,1)}), bf16[8,9,2048]{2,1,0:T(8,128)(2,1)S(1)}, u32[]{:S(2)}, u32[]{:S(2)}) async-start(bf16[8,9,2048]{2,1,0:T(8,128)(2,1)} %reshape.263), calls=%async_computation | async-start | bytes 1048576 | tf_op jit(solution)/shard_map/while/body/eval_jaxpr/all_to_all | solution.py:121
  668.5 10.1 %all-to-all-start.3 = ((bf16[8,1,9]{2,1,0:T(2,128)(2,1)}), bf16[8,1,9]{2,1,0:T(2,128)(2,1)S(1)}, u32[]{:S(2)}, u32[]{:S(2)}) async-start(bf16[8,1,9]{2,1,0:T(2,128)(2,1)} %convert_element_type.181), calls=%async_computation.3 | async-start | bytes 8192 | tf_op jit(solution)/shard_map/while/body/eval_jaxpr/all_to_all | solution.py:141
  678.7 16.9 %all-to-all-start.2 = ((bf16[8,9,2048]{2,1,0:T(8,128)(2,1)}), bf16[8,9,2048]{2,1,0:T(8,128)(2,1)S(1)}, u32[]{:S(2)}, u32[]{:S(2)}) async-start(bf16[8,9,2048]{2,1,0:T(8,128)(2,1)} %reshape.266), calls=%async_computation.2 | async-start | bytes 1048576 | tf_op jit(solution)/shard_map/while/body/eval_jaxpr/all_to_all | solution.py:134
  698.2 29.0 %copy-start.3 = (bf16[2048,8]{0,1:T(8,128)(2,1)S(1)}, bf16[2048,8]{0,1:T(8,128)(2,1)}, u32[]{:S(2)}) copy-start(bf16[2048,8]{0,1:T(8,128)(2,1)} %get-tuple-element.544) | copy-start | bytes 98308 | tf_op jit(solution)/shard_map/while
  698.2 10.1 %collective-permute-start = (bf16[16,2048]{1,0:T(8,128)(2,1)S(1)}, bf16[16,2048]{1,0:T(8,128)(2,1)S(1)}, u32[]{:S(2)}, u32[]{:S(2)}) collective-permute-start(bf16[16,2048]{1,0:T(8,128)(2,1)S(1)} %broadcast_select_fusion.2), channel_id=1, source_target_pairs={{8,0},{16,8},{24,16},{9,1},{17,9},{25,17},{10,2},{18,10},{26,18},{... | collective-permute-start | bytes 196616 | tf_op jit(solution)/shard_map/while/body/eval_jaxpr/ppermute | solution.py:10
  704.7 18.8 %all-to-all-start.1 = ((bf16[8,9,2048]{2,1,0:T(8,128)(2,1)}), bf16[8,9,2048]{2,1,0:T(8,128)(2,1)S(1)}, u32[]{:S(2)}, u32[]{:S(2)}) async-start(bf16[8,9,2048]{2,1,0:T(8,128)(2,1)} %reshape.265), calls=%async_computation.1 | async-start | bytes 1048576 | tf_op jit(solution)/shard_map/while/body/eval_jaxpr/all_to_all | solution.py:120
  723.6 18.3 %all-to-all-start = ((bf16[8,9,2048]{2,1,0:T(8,128)(2,1)}), bf16[8,9,2048]{2,1,0:T(8,128)(2,1)S(1)}, u32[]{:S(2)}, u32[]{:S(2)}) async-start(bf16[8,9,2048]{2,1,0:T(8,128)(2,1)} %reshape.263), calls=%async_computation | async-start | bytes 1048576 | tf_op jit(solution)/shard_map/while/body/eval_jaxpr/all_to_all | solution.py:121
  756.7 10.1 %all-to-all-start.3 = ((bf16[8,1,9]{2,1,0:T(2,128)(2,1)}), bf16[8,1,9]{2,1,0:T(2,128)(2,1)S(1)}, u32[]{:S(2)}, u32[]{:S(2)}) async-start(bf16[8,1,9]{2,1,0:T(2,128)(2,1)} %convert_element_type.181), calls=%async_computation.3 | async-start | bytes 8192 | tf_op jit(solution)/shard_map/while/body/eval_jaxpr/all_to_all | solution.py:141
  766.8 13.7 %all-to-all-start.2 = ((bf16[8,9,2048]{2,1,0:T(8,128)(2,1)}), bf16[8,9,2048]{2,1,0:T(8,128)(2,1)S(1)}, u32[]{:S(2)}, u32[]{:S(2)}) async-start(bf16[8,9,2048]{2,1,0:T(8,128)(2,1)} %reshape.266), calls=%async_computation.2 | async-start | bytes 1048576 | tf_op jit(solution)/shard_map/while/body/eval_jaxpr/all_to_all | solution.py:134
  783.2 29.0 %copy-start.3 = (bf16[2048,8]{0,1:T(8,128)(2,1)S(1)}, bf16[2048,8]{0,1:T(8,128)(2,1)}, u32[]{:S(2)}) copy-start(bf16[2048,8]{0,1:T(8,128)(2,1)} %get-tuple-element.544) | copy-start | bytes 98308 | tf_op jit(solution)/shard_map/while
  783.2 10.1 %collective-permute-start = (bf16[16,2048]{1,0:T(8,128)(2,1)S(1)}, bf16[16,2048]{1,0:T(8,128)(2,1)S(1)}, u32[]{:S(2)}, u32[]{:S(2)}) collective-permute-start(bf16[16,2048]{1,0:T(8,128)(2,1)S(1)} %broadcast_select_fusion.2), channel_id=1, source_target_pairs={{8,0},{16,8},{24,16},{9,1},{17,9},{25,17},{10,2},{18,10},{26,18},{... | collective-permute-start | bytes 196616 | tf_op jit(solution)/shard_map/while/body/eval_jaxpr/ppermute | solution.py:10
  789.6 18.8 %all-to-all-start.1 = ((bf16[8,9,2048]{2,1,0:T(8,128)(2,1)}), bf16[8,9,2048]{2,1,0:T(8,128)(2,1)S(1)}, u32[]{:S(2)}, u32[]{:S(2)}) async-start(bf16[8,9,2048]{2,1,0:T(8,128)(2,1)} %reshape.265), calls=%async_computation.1 | async-start | bytes 1048576 | tf_op jit(solution)/shard_map/while/body/eval_jaxpr/all_to_all | solution.py:120
  808.5 18.3 %all-to-all-start = ((bf16[8,9,2048]{2,1,0:T(8,128)(2,1)}), bf16[8,9,2048]{2,1,0:T(8,128)(2,1)S(1)}, u32[]{:S(2)}, u32[]{:S(2)}) async-start(bf16[8,9,2048]{2,1,0:T(8,128)(2,1)} %reshape.263), calls=%async_computation | async-start | bytes 1048576 | tf_op jit(solution)/shard_map/while/body/eval_jaxpr/all_to_all | solution.py:121
  827.5 10.1 %all-to-all-start.3 = ((bf16[8,1,9]{2,1,0:T(2,128)(2,1)}), bf16[8,1,9]{2,1,0:T(2,128)(2,1)S(1)}, u32[]{:S(2)}, u32[]{:S(2)}) async-start(bf16[8,1,9]{2,1,0:T(2,128)(2,1)} %convert_element_type.181), calls=%async_computation.3 | async-start | bytes 8192 | tf_op jit(solution)/shard_map/while/body/eval_jaxpr/all_to_all | solution.py:141
  837.7 16.9 %all-to-all-start.2 = ((bf16[8,9,2048]{2,1,0:T(8,128)(2,1)}), bf16[8,9,2048]{2,1,0:T(8,128)(2,1)S(1)}, u32[]{:S(2)}, u32[]{:S(2)}) async-start(bf16[8,9,2048]{2,1,0:T(8,128)(2,1)} %reshape.266), calls=%async_computation.2 | async-start | bytes 1048576 | tf_op jit(solution)/shard_map/while/body/eval_jaxpr/all_to_all | solution.py:134
  857.3 10.1 %collective-permute-start = (bf16[16,2048]{1,0:T(8,128)(2,1)S(1)}, bf16[16,2048]{1,0:T(8,128)(2,1)S(1)}, u32[]{:S(2)}, u32[]{:S(2)}) collective-permute-start(bf16[16,2048]{1,0:T(8,128)(2,1)S(1)} %broadcast_select_fusion.2), channel_id=1, source_target_pairs={{8,0},{16,8},{24,16},{9,1},{17,9},{25,17},{10,2},{18,10},{26,18},{... | collective-permute-start | bytes 196616 | tf_op jit(solution)/shard_map/while/body/eval_jaxpr/ppermute | solution.py:10
  863.7 18.8 %all-to-all-start.1 = ((bf16[8,9,2048]{2,1,0:T(8,128)(2,1)}), bf16[8,9,2048]{2,1,0:T(8,128)(2,1)S(1)}, u32[]{:S(2)}, u32[]{:S(2)}) async-start(bf16[8,9,2048]{2,1,0:T(8,128)(2,1)} %reshape.265), calls=%async_computation.1 | async-start | bytes 1048576 | tf_op jit(solution)/shard_map/while/body/eval_jaxpr/all_to_all | solution.py:120
  882.6 18.3 %all-to-all-start = ((bf16[8,9,2048]{2,1,0:T(8,128)(2,1)}), bf16[8,9,2048]{2,1,0:T(8,128)(2,1)S(1)}, u32[]{:S(2)}, u32[]{:S(2)}) async-start(bf16[8,9,2048]{2,1,0:T(8,128)(2,1)} %reshape.263), calls=%async_computation | async-start | bytes 1048576 | tf_op jit(solution)/shard_map/while/body/eval_jaxpr/all_to_all | solution.py:121
  901.6 10.1 %all-to-all-start.3 = ((bf16[8,1,9]{2,1,0:T(2,128)(2,1)}), bf16[8,1,9]{2,1,0:T(2,128)(2,1)S(1)}, u32[]{:S(2)}, u32[]{:S(2)}) async-start(bf16[8,1,9]{2,1,0:T(2,128)(2,1)} %convert_element_type.181), calls=%async_computation.3 | async-start | bytes 8192 | tf_op jit(solution)/shard_map/while/body/eval_jaxpr/all_to_all | solution.py:141
  911.7 16.9 %all-to-all-start.2 = ((bf16[8,9,2048]{2,1,0:T(8,128)(2,1)}), bf16[8,9,2048]{2,1,0:T(8,128)(2,1)S(1)}, u32[]{:S(2)}, u32[]{:S(2)}) async-start(bf16[8,9,2048]{2,1,0:T(8,128)(2,1)} %reshape.266), calls=%async_computation.2 | async-start | bytes 1048576 | tf_op jit(solution)/shard_map/while/body/eval_jaxpr/all_to_all | solution.py:134
  (27 other events, 161.2 us)
where the time goes:
time: 939 us; the launch traced here: 932 us
  waiting for transfers between devices  498 us (53%)
  starting transfers between devices  189 us (20%)
  matrix products  138 us (15%)
  local copies, waits for them, and re-layouts  60.3 us (6%)
  other arithmetic  37.8 us (4%)
    all_to_all x11, waiting for transfers between devices, advance(): lax.all_to_all(sent_grad, 'expert', split_axis=0, concat_axis=0, tiled=True)  155 us
    all_to_all x11, waiting for transfers between devices, advance(): lax.all_to_all(sent_normed, 'expert', split_axis=0, concat_axis=0, tiled=...  144 us
    all_to_all x11, waiting for transfers between devices, advance(): lax.all_to_all(returned.reshape(experts, capacity, width), 'expert', spli...  139 us
    all_to_all x11, waiting for transfers between devices, advance(): lax.all_to_all(dprob.reshape(experts, capacity).astype(jnp.bfloat16), 'ex...  58.5 us
    all_to_all x11, starting transfers between devices, advance(): lax.all_to_all(sent_normed, 'expert', split_axis=0, concat_axis=0, tiled=...  43.6 us
    all_to_all x11, starting transfers between devices, advance(): lax.all_to_all(dprob.reshape(experts, capacity).astype(jnp.bfloat16), 'ex...  42.3 us
    all_to_all x11, starting transfers between devices, advance(): lax.all_to_all(sent_grad, 'expert', split_axis=0, concat_axis=0, tiled=True)  39.9 us
    all_to_all x11, starting transfers between devices, advance(): lax.all_to_all(returned.reshape(experts, capacity, width), 'expert', spli...  38.4 us
  transfers between devices with their start and end apart: 55, of which 45 were waited for; matrix products, arithmetic and copies ran while one was open for 9% of the time, Pallas kernels for 0%

commit v1 on v0

--- a/solution.py
+++ b/solution.py
@@ -2,6 +2,29 @@
 import jax.numpy as jnp
 from jax import lax
 from jax.sharding import PartitionSpec as P
+
+
+def cut_along(x, dim, size):
+    lengths = x.shape
+    blocks = x.reshape(*lengths[:dim], size, lengths[dim] // size, *lengths[dim + 1 :])
+    return jnp.moveaxis(blocks, dim, 0)
+
+
+def joined_along(parts, dim):
+    parts = jnp.moveaxis(parts, 0, dim)
+    lengths = parts.shape
+    return parts.reshape(*lengths[:dim], lengths[dim] * lengths[dim + 1], *lengths[dim + 2 :])
+
+
+def sent_to_each(x, axis, split_dim, concat_dim):
+    peers, index = (lax.axis_size(axis), lax.axis_index(axis))
+    blocks = cut_along(x, split_dim, peers)
+    outs = [blocks[index]]
+    for hop in range(1, peers):
+        sent = blocks[(index + hop) % peers]
+        outs.append(lax.ppermute(sent, axis, [(i, (i + hop) % peers) for i in range(peers)]))
+    blocks = jnp.stack(outs)[(index - jnp.arange(peers)) % peers]
+    return joined_along(blocks, concat_dim)
 
 
 def shifted(shard, axis, by):
@@ -117,7 +140,7 @@
         sent_normed = pack_rows(select, normed, per_token).reshape(experts, capacity, width)
         sent_grad = pack_rows(select, grad_in, per_token).reshape(experts, capacity, width)
         got_normed, got_grad = (
-            lax.all_to_all(sent_normed, "expert", split_axis=0, concat_axis=0, tiled=True),
+            sent_to_each(sent_normed, "expert", 0, 0),
             lax.all_to_all(sent_grad, "expert", split_axis=0, concat_axis=0, tiled=True),
         )
         rows_normed = got_normed.reshape(slots, width)

time: 939 us -> 886 us (0.944)
  waiting for transfers between devices: 498 us -> 368 us
  starting transfers between devices: 189 us -> 257 us
  local copies, waits for them, and re-layouts: 60.3 us -> 69.8 us
    all_to_all x11 -> x0, waiting for transfers between devices: 144 us -> none  [advance(): lax.all_to_all(sent_normed, 'expert', split_axis=0, concat_axis=0, tiled=...]
    ppermute x0 -> x77, starting transfers between devices: none -> 108 us  [sent_to_each(): lax.ppermute(sent, axis, [(i, (i + hop) % peers) for i in range(peers)])]
    all_to_all x11 -> x0, starting transfers between devices: 43.6 us -> none  [advance(): lax.all_to_all(sent_normed, 'expert', split_axis=0, concat_axis=0, tiled=...]
    ppermute x0 -> x77, waiting for transfers between devices: none -> 43.3 us  [sent_to_each(): lax.ppermute(sent, axis, [(i, (i + hop) % peers) for i in range(peers)])]
    dot_general x8, matrix products: 25.6 us -> 6.81 us  [expert_rows(): up_rows = jnp.dot(normed_rows, up_w, preferred_element_type=jnp.float32)]
    dot_general x8, matrix products: 7.72 us -> 26.2 us  [expert_rows(): output = jnp.dot(hidden, down_w, preferred_element_type=jnp.float32)]
    all_to_all x11, waiting for transfers between devices: 155 us -> 138 us  [advance(): lax.all_to_all(sent_grad, 'expert', split_axis=0, concat_axis=0, tiled=True)]
    dot_general x8, matrix products: 28.7 us -> 11.2 us  [expert_rows(): lax.dot_general(grad_rows, down_w, (((1,), (1,)), ((), ())), preferred_el...]
  transfers between devices with their start and end apart: 55 -> 121, of which waited for: 45 -> 54; matrix products, arithmetic and copies ran while one was open for 9% -> 11% of each run, Pallas kernels for 0% -> 0%
where the time goes in v1:
time: 886 us; the launch traced here: 879 us
  waiting for transfers between devices  368 us (42%)
  starting transfers between devices  257 us (29%)
  matrix products  129 us (15%)
  local copies, waits for them, and re-layouts  69.8 us (8%)
  other arithmetic  44.9 us (5%)
    all_to_all x11, waiting for transfers between devices, advance(): lax.all_to_all(sent_grad, 'expert', split_axis=0, concat_axis=0, tiled=True)  138 us
    all_to_all x11, waiting for transfers between devices, advance(): lax.all_to_all(returned.reshape(experts, capacity, width), 'expert', spli...  128 us
    ppermute x77, starting transfers between devices, sent_to_each(): lax.ppermute(sent, axis, [(i, (i + hop) % peers) for i in range(peers)])  108 us
    all_to_all x11, waiting for transfers between devices, advance(): lax.all_to_all(dprob.reshape(experts, capacity).astype(jnp.bfloat16), 'ex...  58.5 us
    all_to_all x11, starting transfers between devices, advance(): lax.all_to_all(sent_grad, 'expert', split_axis=0, concat_axis=0, tiled=True)  44.5 us
    ppermute x77, waiting for transfers between devices, sent_to_each(): lax.ppermute(sent, axis, [(i, (i + hop) % peers) for i in range(peers)])  43.3 us
    all_to_all x11, starting transfers between devices, advance(): lax.all_to_all(dprob.reshape(experts, capacity).astype(jnp.bfloat16), 'ex...  43.3 us
    all_to_all x11, starting transfers between devices, advance(): lax.all_to_all(returned.reshape(experts, capacity, width), 'expert', spli...  38.4 us
  transfers between devices with their start and end apart: 121, of which 54 were waited for; matrix products, arithmetic and copies ran while one was open for 11% of the time, Pallas kernels for 0%

profile of v1, /device:TPU:2, one launch (start us, length us, event | category | flops | bytes accessed | tf_op | source)
XLA Modules:
  0.0 879.5 jit_solution(1746470085335953606)
XLA Ops:
  2.2 7.0 all_gather.3
  10.0 869.5 %while.18 = (s32[]{:T(128)}, bf16[16,2048]{1,0:T(8,128)(2,1)S(1)}, bf16[8,16,2048]{2,1,0:T(8,128)(2,1)}, pred[]{:T(512)}, s32[]{:T(128)}, /*index=5*/bf16[8,16,2...) while((s32[]{:T(128)}, bf16[16,2048]{1,0:T(8,128)(2,1)S(1)}, ...), condition=%wide.region_13.14_spmd.clone, body=%wide.region_0.13_spmd.clone.sunk | while | flops 1876002688 | bytes 112725904 | solution.py:196
  33.7 4.4 all-to-all-start
  38.1 12.0 %all-to-all-done = bf16[8,9,2048]{2,1,0:T(8,128)(2,1)S(1)} async-done(((bf16[8,9,2048]{2,1,0:T(8,128)(2,1)}), bf16[8,9,2048]{2,1,0:T(8,128)(2,1)S(1)}, u32[]{:S(2)}, u32[]{:S(2)}) %all-to-all-start) | async-done | bytes 294944 | tf_op jit(solution)/shard_map/while/body/eval_jaxpr/all_to_all | solution.py:144
  50.8 3.7 all-to-all-start.2
  55.7 5.3 all-to-all-done.2
  64.9 9.8 %all-to-all-done.1 = bf16[8,9,2048]{2,1,0:T(8,128)(2,1)S(1)} async-done(((bf16[8,9,2048]{2,1,0:T(8,128)(2,1)}), bf16[8,9,2048]{2,1,0:T(8,128)(2,1)S(1)}, u32[]{:S(2)}, u32[]{:S(2)}) %all-to-all-start.1) | async-done | bytes 294944 | tf_op jit(solution)/shard_map/while/body/eval_jaxpr/all_to_all | solution.py:157
  92.7 3.8 collective-permute-start.5
  101.0 5.0 all-to-all-start
  106.0 11.4 %all-to-all-done = bf16[8,9,2048]{2,1,0:T(8,128)(2,1)S(1)} async-done(((bf16[8,9,2048]{2,1,0:T(8,128)(2,1)}), bf16[8,9,2048]{2,1,0:T(8,128)(2,1)S(1)}, u32[]{:S(2)}, u32[]{:S(2)}) %all-to-all-start) | async-done | bytes 294944 | tf_op jit(solution)/shard_map/while/body/eval_jaxpr/all_to_all | solution.py:144
  117.5 12.9 %conditional.3 = (bf16[72,2048]{1,0:T(8,128)(2,1)S(1)}, bf16[72]{0:T(256)(128)(2,1)S(1)}) conditional(s32[]{:T(128)} %convert_element_type.195, () %tuple.85, (bf16[8,9,2048]{2,1,0:T(8,128)(2,1)S(1)}, bf16[1024,2048]{1,0:T(8,128)(2,1)}, s32[]{:T(128)}, s32[8,1]{0,1:T(1,128)S(1)}, s32[]{:T(128)}, ...), branch_computations={%region_6.6_spmd, %region_7.8_spmd.clone} | conditional | flops 1814299648 | bytes 99651992 | solution.py:155
  131.1 7.2 all-to-all-start.2
  139.5 5.3 all-to-all-done.2
  148.7 13.7 %all-to-all-done.1 = bf16[8,9,2048]{2,1,0:T(8,128)(2,1)S(1)} async-done(((bf16[8,9,2048]{2,1,0:T(8,128)(2,1)}), bf16[8,9,2048]{2,1,0:T(8,128)(2,1)S(1)}, u32[]{:S(2)}, u32[]{:S(2)}) %all-to-all-start.1) | async-done | bytes 294944 | tf_op jit(solution)/shard_map/while/body/eval_jaxpr/all_to_all | solution.py:157
  188.7 3.9 all-to-all-start
  192.6 12.7 %all-to-all-done = bf16[8,9,2048]{2,1,0:T(8,128)(2,1)S(1)} async-done(((bf16[8,9,2048]{2,1,0:T(8,128)(2,1)}), bf16[8,9,2048]{2,1,0:T(8,128)(2,1)S(1)}, u32[]{:S(2)}, u32[]{:S(2)}) %all-to-all-start) | async-done | bytes 294944 | tf_op jit(solution)/shard_map/while/body/eval_jaxpr/all_to_all | solution.py:144
  205.4 12.9 %conditional.3 = (bf16[72,2048]{1,0:T(8,128)(2,1)S(1)}, bf16[72]{0:T(256)(128)(2,1)S(1)}) conditional(s32[]{:T(128)} %convert_element_type.195, () %tuple.85, (bf16[8,9,2048]{2,1,0:T(8,128)(2,1)S(1)}, bf16[1024,2048]{1,0:T(8,128)(2,1)}, s32[]{:T(128)}, s32[8,1]{0,1:T(1,128)S(1)}, s32[]{:T(128)}, ...), branch_computations={%region_6.6_spmd, %region_7.8_spmd.clone} | conditional | flops 1814299648 | bytes 99651992 | solution.py:155
  223.8 5.3 all-to-all-done.2
  233.0 11.9 %all-to-all-done.1 = bf16[8,9,2048]{2,1,0:T(8,128)(2,1)S(1)} async-done(((bf16[8,9,2048]{2,1,0:T(8,128)(2,1)}), bf16[8,9,2048]{2,1,0:T(8,128)(2,1)S(1)}, u32[]{:S(2)}, u32[]{:S(2)}) %all-to-all-start.1) | async-done | bytes 294944 | tf_op jit(solution)/shard_map/while/body/eval_jaxpr/all_to_all | solution.py:157
  271.1 3.9 all-to-all-start
  275.1 12.7 %all-to-all-done = bf16[8,9,2048]{2,1,0:T(8,128)(2,1)S(1)} async-done(((bf16[8,9,2048]{2,1,0:T(8,128)(2,1)}), bf16[8,9,2048]{2,1,0:T(8,128)(2,1)S(1)}, u32[]{:S(2)}, u32[]{:S(2)}) %all-to-all-start) | async-done | bytes 294944 | tf_op jit(solution)/shard_map/while/body/eval_jaxpr/all_to_all | solution.py:144
  287.8 12.9 %conditional.3 = (bf16[72,2048]{1,0:T(8,128)(2,1)S(1)}, bf16[72]{0:T(256)(128)(2,1)S(1)}) conditional(s32[]{:T(128)} %convert_element_type.195, () %tuple.85, (bf16[8,9,2048]{2,1,0:T(8,128)(2,1)S(1)}, bf16[1024,2048]{1,0:T(8,128)(2,1)}, s32[]{:T(128)}, s32[8,1]{0,1:T(1,128)S(1)}, s32[]{:T(128)}, ...), branch_computations={%region_6.6_spmd, %region_7.8_spmd.clone} | conditional | flops 1814299648 | bytes 99651992 | solution.py:155
  301.4 3.6 all-to-all-start.2
  306.2 5.3 all-to-all-done.2
  315.4 11.9 %all-to-all-done.1 = bf16[8,9,2048]{2,1,0:T(8,128)(2,1)S(1)} async-done(((bf16[8,9,2048]{2,1,0:T(8,128)(2,1)}), bf16[8,9,2048]{2,1,0:T(8,128)(2,1)S(1)}, u32[]{:S(2)}, u32[]{:S(2)}) %all-to-all-start.1) | async-done | bytes 294944 | tf_op jit(solution)/shard_map/while/body/eval_jaxpr/all_to_all | solution.py:157
  353.5 3.9 all-to-all-start
  357.5 12.7 %all-to-all-done = bf16[8,9,2048]{2,1,0:T(8,128)(2,1)S(1)} async-done(((bf16[8,9,2048]{2,1,0:T(8,128)(2,1)}), bf16[8,9,2048]{2,1,0:T(8,128)(2,1)S(1)}, u32[]{:S(2)}, u32[]{:S(2)}) %all-to-all-start) | async-done | bytes 294944 | tf_op jit(solution)/shard_map/while/body/eval_jaxpr/all_to_all | solution.py:144
  370.2 12.9 %conditional.3 = (bf16[72,2048]{1,0:T(8,128)(2,1)S(1)}, bf16[72]{0:T(256)(128)(2,1)S(1)}) conditional(s32[]{:T(128)} %convert_element_type.195, () %tuple.85, (bf16[8,9,2048]{2,1,0:T(8,128)(2,1)S(1)}, bf16[1024,2048]{1,0:T(8,128)(2,1)}, s32[]{:T(128)}, s32[8,1]{0,1:T(1,128)S(1)}, s32[]{:T(128)}, ...), branch_computations={%region_6.6_spmd, %region_7.8_spmd.clone} | conditional | flops 1814299648 | bytes 99651992 | solution.py:155
  383.8 3.6 all-to-all-start.2
  388.6 5.3 all-to-all-done.2
  397.8 11.9 %all-to-all-done.1 = bf16[8,9,2048]{2,1,0:T(8,128)(2,1)S(1)} async-done(((bf16[8,9,2048]{2,1,0:T(8,128)(2,1)}), bf16[8,9,2048]{2,1,0:T(8,128)(2,1)S(1)}, u32[]{:S(2)}, u32[]{:S(2)}) %all-to-all-start.1) | async-done | bytes 294944 | tf_op jit(solution)/shard_map/while/body/eval_jaxpr/all_to_all | solution.py:157
  435.9 3.9 all-to-all-start
  439.9 12.7 %all-to-all-done = bf16[8,9,2048]{2,1,0:T(8,128)(2,1)S(1)} async-done(((bf16[8,9,2048]{2,1,0:T(8,128)(2,1)}), bf16[8,9,2048]{2,1,0:T(8,128)(2,1)S(1)}, u32[]{:S(2)}, u32[]{:S(2)}) %all-to-all-start) | async-done | bytes 294944 | tf_op jit(solution)/shard_map/while/body/eval_jaxpr/all_to_all | solution.py:144
  452.6 12.9 %conditional.3 = (bf16[72,2048]{1,0:T(8,128)(2,1)S(1)}, bf16[72]{0:T(256)(128)(2,1)S(1)}) conditional(s32[]{:T(128)} %convert_element_type.195, () %tuple.85, (bf16[8,9,2048]{2,1,0:T(8,128)(2,1)S(1)}, bf16[1024,2048]{1,0:T(8,128)(2,1)}, s32[]{:T(128)}, s32[8,1]{0,1:T(1,128)S(1)}, s32[]{:T(128)}, ...), branch_computations={%region_6.6_spmd, %region_7.8_spmd.clone} | conditional | flops 1814299648 | bytes 99651992 | solution.py:155
  466.2 3.6 all-to-all-start.2
  471.0 5.3 all-to-all-done.2
  480.2 11.9 %all-to-all-done.1 = bf16[8,9,2048]{2,1,0:T(8,128)(2,1)S(1)} async-done(((bf16[8,9,2048]{2,1,0:T(8,128)(2,1)}), bf16[8,9,2048]{2,1,0:T(8,128)(2,1)S(1)}, u32[]{:S(2)}, u32[]{:S(2)}) %all-to-all-start.1) | async-done | bytes 294944 | tf_op jit(solution)/shard_map/while/body/eval_jaxpr/all_to_all | solution.py:157
  518.3 3.9 all-to-all-start
  522.3 12.7 %all-to-all-done = bf16[8,9,2048]{2,1,0:T(8,128)(2,1)S(1)} async-done(((bf16[8,9,2048]{2,1,0:T(8,128)(2,1)}), bf16[8,9,2048]{2,1,0:T(8,128)(2,1)S(1)}, u32[]{:S(2)}, u32[]{:S(2)}) %all-to-all-start) | async-done | bytes 294944 | tf_op jit(solution)/shard_map/while/body/eval_jaxpr/all_to_all | solution.py:144
  535.0 12.9 %conditional.3 = (bf16[72,2048]{1,0:T(8,128)(2,1)S(1)}, bf16[72]{0:T(256)(128)(2,1)S(1)}) conditional(s32[]{:T(128)} %convert_element_type.195, () %tuple.85, (bf16[8,9,2048]{2,1,0:T(8,128)(2,1)S(1)}, bf16[1024,2048]{1,0:T(8,128)(2,1)}, s32[]{:T(128)}, s32[8,1]{0,1:T(1,128)S(1)}, s32[]{:T(128)}, ...), branch_computations={%region_6.6_spmd, %region_7.8_spmd.clone} | conditional | flops 1814299648 | bytes 99651992 | solution.py:155
  548.6 3.6 all-to-all-start.2
  553.4 5.3 all-to-all-done.2
  562.6 11.9 %all-to-all-done.1 = bf16[8,9,2048]{2,1,0:T(8,128)(2,1)S(1)} async-done(((bf16[8,9,2048]{2,1,0:T(8,128)(2,1)}), bf16[8,9,2048]{2,1,0:T(8,128)(2,1)S(1)}, u32[]{:S(2)}, u32[]{:S(2)}) %all-to-all-start.1) | async-done | bytes 294944 | tf_op jit(solution)/shard_map/while/body/eval_jaxpr/all_to_all | solution.py:157
  600.7 3.9 all-to-all-start
  604.7 12.7 %all-to-all-done = bf16[8,9,2048]{2,1,0:T(8,128)(2,1)S(1)} async-done(((bf16[8,9,2048]{2,1,0:T(8,128)(2,1)}), bf16[8,9,2048]{2,1,0:T(8,128)(2,1)S(1)}, u32[]{:S(2)}, u32[]{:S(2)}) %all-to-all-start) | async-done | bytes 294944 | tf_op jit(solution)/shard_map/while/body/eval_jaxpr/all_to_all | solution.py:144
  617.4 12.9 %conditional.3 = (bf16[72,2048]{1,0:T(8,128)(2,1)S(1)}, bf16[72]{0:T(256)(128)(2,1)S(1)}) conditional(s32[]{:T(128)} %convert_element_type.195, () %tuple.85, (bf16[8,9,2048]{2,1,0:T(8,128)(2,1)S(1)}, bf16[1024,2048]{1,0:T(8,128)(2,1)}, s32[]{:T(128)}, s32[8,1]{0,1:T(1,128)S(1)}, s32[]{:T(128)}, ...), branch_computations={%region_6.6_spmd, %region_7.8_spmd.clone} | conditional | flops 1814299648 | bytes 99651992 | solution.py:155
  631.0 3.6 all-to-all-start.2
  635.8 5.3 all-to-all-done.2
  645.0 11.9 %all-to-all-done.1 = bf16[8,9,2048]{2,1,0:T(8,128)(2,1)S(1)} async-done(((bf16[8,9,2048]{2,1,0:T(8,128)(2,1)}), bf16[8,9,2048]{2,1,0:T(8,128)(2,1)S(1)}, u32[]{:S(2)}, u32[]{:S(2)}) %all-to-all-start.1) | async-done | bytes 294944 | tf_op jit(solution)/shard_map/while/body/eval_jaxpr/all_to_all | solution.py:157
  683.1 3.9 all-to-all-start
  687.1 12.7 %all-to-all-done = bf16[8,9,2048]{2,1,0:T(8,128)(2,1)S(1)} async-done(((bf16[8,9,2048]{2,1,0:T(8,128)(2,1)}), bf16[8,9,2048]{2,1,0:T(8,128)(2,1)S(1)}, u32[]{:S(2)}, u32[]{:S(2)}) %all-to-all-start) | async-done | bytes 294944 | tf_op jit(solution)/shard_map/while/body/eval_jaxpr/all_to_all | solution.py:144
  699.8 12.9 %conditional.3 = (bf16[72,2048]{1,0:T(8,128)(2,1)S(1)}, bf16[72]{0:T(256)(128)(2,1)S(1)}) conditional(s32[]{:T(128)} %convert_element_type.195, () %tuple.85, (bf16[8,9,2048]{2,1,0:T(8,128)(2,1)S(1)}, bf16[1024,2048]{1,0:T(8,128)(2,1)}, s32[]{:T(128)}, s32[8,1]{0,1:T(1,128)S(1)}, s32[]{:T(128)}, ...), branch_computations={%region_6.6_spmd, %region_7.8_spmd.clone} | conditional | flops 1814299648 | bytes 99651992 | solution.py:155
  713.4 3.6 all-to-all-start.2
  718.2 5.3 all-to-all-done.2
  727.4 9.8 %all-to-all-done.1 = bf16[8,9,2048]{2,1,0:T(8,128)(2,1)S(1)} async-done(((bf16[8,9,2048]{2,1,0:T(8,128)(2,1)}), bf16[8,9,2048]{2,1,0:T(8,128)(2,1)S(1)}, u32[]{:S(2)}, u32[]{:S(2)}) %all-to-all-start.1) | async-done | bytes 294944 | tf_op jit(solution)/shard_map/while/body/eval_jaxpr/all_to_all | solution.py:157
  763.5 3.9 all-to-all-start
  767.4 12.7 %all-to-all-done = bf16[8,9,2048]{2,1,0:T(8,128)(2,1)S(1)} async-done(((bf16[8,9,2048]{2,1,0:T(8,128)(2,1)}), bf16[8,9,2048]{2,1,0:T(8,128)(2,1)S(1)}, u32[]{:S(2)}, u32[]{:S(2)}) %all-to-all-start) | async-done | bytes 294944 | tf_op jit(solution)/shard_map/while/body/eval_jaxpr/all_to_all | solution.py:144
  785.6 5.3 all-to-all-done.2
  794.8 11.8 %all-to-all-done.1 = bf16[8,9,2048]{2,1,0:T(8,128)(2,1)S(1)} async-done(((bf16[8,9,2048]{2,1,0:T(8,128)(2,1)}), bf16[8,9,2048]{2,1,0:T(8,128)(2,1)S(1)}, u32[]{:S(2)}, u32[]{:S(2)}) %all-to-all-start.1) | async-done | bytes 294944 | tf_op jit(solution)/shard_map/while/body/eval_jaxpr/all_to_all | solution.py:157
  832.9 3.9 all-to-all-start
  836.9 12.7 %all-to-all-done = bf16[8,9,2048]{2,1,0:T(8,128)(2,1)S(1)} async-done(((bf16[8,9,2048]{2,1,0:T(8,128)(2,1)}), bf16[8,9,2048]{2,1,0:T(8,128)(2,1)S(1)}, u32[]{:S(2)}, u32[]{:S(2)}) %all-to-all-start) | async-done | bytes 294944 | tf_op jit(solution)/shard_map/while/body/eval_jaxpr/all_to_all | solution.py:144
  850.3 3.6 all-to-all-start.2
  855.1 5.3 all-to-all-done.2
  864.3 11.9 %all-to-all-done.1 = bf16[8,9,2048]{2,1,0:T(8,128)(2,1)S(1)} async-done(((bf16[8,9,2048]{2,1,0:T(8,128)(2,1)}), bf16[8,9,2048]{2,1,0:T(8,128)(2,1)S(1)}, u32[]{:S(2)}, u32[]{:S(2)}) %all-to-all-start.1) | async-done | bytes 294944 | tf_op jit(solution)/shard_map/while/body/eval_jaxpr/all_to_all | solution.py:157
  (892 shorter events, 459.1 us)
Async XLA Ops:
  10.0 22.3 %collective-permute-start = (bf16[16,2048]{1,0:T(8,128)(2,1)S(1)}, bf16[16,2048]{1,0:T(8,128)(2,1)S(1)}, u32[]{:S(2)}, u32[]{:S(2)}) collective-permute-start(bf16[16,2048]{1,0:T(8,128)(2,1)S(1)} %broadcast_select_fusion.2), channel_id=1, source_target_pairs={{8,0},{16,8},{24,16},{9,1},{17,9},{25,17},{10,2},{18,10},{26,18},{... | collective-permute-start | bytes 196616 | tf_op jit(solution)/shard_map/while/body/eval_jaxpr/ppermute | solution.py:33
  33.7 16.4 %all-to-all-start = ((bf16[8,9,2048]{2,1,0:T(8,128)(2,1)}), bf16[8,9,2048]{2,1,0:T(8,128)(2,1)S(1)}, u32[]{:S(2)}, u32[]{:S(2)}) async-start(bf16[8,9,2048]{2,1,0:T(8,128)(2,1)} %reshape.303), calls=%async_computation | async-start | bytes 1048576 | tf_op jit(solution)/shard_map/while/body/eval_jaxpr/all_to_all | solution.py:144
  50.8 10.2 %all-to-all-start.2 = ((bf16[8,1,9]{2,1,0:T(2,128)(2,1)}), bf16[8,1,9]{2,1,0:T(2,128)(2,1)S(1)}, u32[]{:S(2)}, u32[]{:S(2)}) async-start(bf16[8,1,9]{2,1,0:T(2,128)(2,1)} %convert_element_type.196), calls=%async_computation.2 | async-start | bytes 8192 | tf_op jit(solution)/shard_map/while/body/eval_jaxpr/all_to_all | solution.py:164
  61.0 13.7 %all-to-all-start.1 = ((bf16[8,9,2048]{2,1,0:T(8,128)(2,1)}), bf16[8,9,2048]{2,1,0:T(8,128)(2,1)S(1)}, u32[]{:S(2)}, u32[]{:S(2)}) async-start(bf16[8,9,2048]{2,1,0:T(8,128)(2,1)} %reshape.306), calls=%async_computation.1 | async-start | bytes 1048576 | tf_op jit(solution)/shard_map/while/body/eval_jaxpr/all_to_all | solution.py:157
  78.0 21.5 %collective-permute-start = (bf16[16,2048]{1,0:T(8,128)(2,1)S(1)}, bf16[16,2048]{1,0:T(8,128)(2,1)S(1)}, u32[]{:S(2)}, u32[]{:S(2)}) collective-permute-start(bf16[16,2048]{1,0:T(8,128)(2,1)S(1)} %broadcast_select_fusion.2), channel_id=1, source_target_pairs={{8,0},{16,8},{24,16},{9,1},{17,9},{25,17},{10,2},{18,10},{26,18},{... | collective-permute-start | bytes 196616 | tf_op jit(solution)/shard_map/while/body/eval_jaxpr/ppermute | solution.py:33
  86.4 10.1 %collective-permute-start.2 = (bf16[1,9,2048]{2,1,0:T(8,128)(2,1)S(1)}, bf16[1,9,2048]{2,1,0:T(8,128)(2,1)S(1)}, u32[]{:S(2)}, u32[]{:S(2)}) collective-permute-start(bf16[1,9,2048]{2,1,0:T(8,128)(2,1)S(1)} %get-tuple-element.646), channel_id=1, source_target_pairs={{0,2},{1,3},{2,4},{3,5},{4,6},{5,7},{6,0},{7,1},{8,10},{9,11},{10,... | collective-permute-start | bytes 110600 | tf_op jit(solution)/shard_map/while/body/eval_jaxpr/ppermute | solution.py:25
  101.0 16.5 %all-to-all-start = ((bf16[8,9,2048]{2,1,0:T(8,128)(2,1)}), bf16[8,9,2048]{2,1,0:T(8,128)(2,1)S(1)}, u32[]{:S(2)}, u32[]{:S(2)}) async-start(bf16[8,9,2048]{2,1,0:T(8,128)(2,1)} %reshape.303), calls=%async_computation | async-start | bytes 1048576 | tf_op jit(solution)/shard_map/while/body/eval_jaxpr/all_to_all | solution.py:144
  131.1 13.7 %all-to-all-start.2 = ((bf16[8,1,9]{2,1,0:T(2,128)(2,1)}), bf16[8,1,9]{2,1,0:T(2,128)(2,1)S(1)}, u32[]{:S(2)}, u32[]{:S(2)}) async-start(bf16[8,1,9]{2,1,0:T(2,128)(2,1)} %convert_element_type.196), calls=%async_computation.2 | async-start | bytes 8192 | tf_op jit(solution)/shard_map/while/body/eval_jaxpr/all_to_all | solution.py:164
  144.8 17.6 %all-to-all-start.1 = ((bf16[8,9,2048]{2,1,0:T(8,128)(2,1)}), bf16[8,9,2048]{2,1,0:T(8,128)(2,1)S(1)}, u32[]{:S(2)}, u32[]{:S(2)}) async-start(bf16[8,9,2048]{2,1,0:T(8,128)(2,1)} %reshape.306), calls=%async_computation.1 | async-start | bytes 1048576 | tf_op jit(solution)/shard_map/while/body/eval_jaxpr/all_to_all | solution.py:157
  165.7 21.5 %collective-permute-start = (bf16[16,2048]{1,0:T(8,128)(2,1)S(1)}, bf16[16,2048]{1,0:T(8,128)(2,1)S(1)}, u32[]{:S(2)}, u32[]{:S(2)}) collective-permute-start(bf16[16,2048]{1,0:T(8,128)(2,1)S(1)} %broadcast_select_fusion.2), channel_id=1, source_target_pairs={{8,0},{16,8},{24,16},{9,1},{17,9},{25,17},{10,2},{18,10},{26,18},{... | collective-permute-start | bytes 196616 | tf_op jit(solution)/shard_map/while/body/eval_jaxpr/ppermute | solution.py:33
  173.1 11.5 %collective-permute-start.3 = (bf16[1,9,2048]{2,1,0:T(8,128)(2,1)S(1)}, bf16[1,9,2048]{2,1,0:T(8,128)(2,1)S(1)}, u32[]{:S(2)}, u32[]{:S(2)}) collective-permute-start(bf16[1,9,2048]{2,1,0:T(8,128)(2,1)S(1)} %get-tuple-element.647), channel_id=1, source_target_pairs={{0,3},{1,4},{2,5},{3,6},{4,7},{5,0},{6,1},{7,2},{8,11},{9,12},{10,... | collective-permute-start | bytes 110600 | tf_op jit(solution)/shard_map/while/body/eval_jaxpr/ppermute | solution.py:25
  180.8 11.8 %collective-permute-start.6 = (bf16[1,9,2048]{2,1,0:T(8,128)(2,1)S(1)}, bf16[1,9,2048]{2,1,0:T(8,128)(2,1)S(1)}, u32[]{:S(2)}, u32[]{:S(2)}) collective-permute-start(bf16[1,9,2048]{2,1,0:T(8,128)(2,1)S(1)} %get-tuple-element.650), channel_id=1, source_target_pairs={{0,6},{1,7},{2,0},{3,1},{4,2},{5,3},{6,4},{7,5},{8,14},{9,15},{10,... | collective-permute-start | bytes 110600 | tf_op jit(solution)/shard_map/while/body/eval_jaxpr/ppermute | solution.py:25
  188.7 16.6 %all-to-all-start = ((bf16[8,9,2048]{2,1,0:T(8,128)(2,1)}), bf16[8,9,2048]{2,1,0:T(8,128)(2,1)S(1)}, u32[]{:S(2)}, u32[]{:S(2)}) async-start(bf16[8,9,2048]{2,1,0:T(8,128)(2,1)} %reshape.303), calls=%async_computation | async-start | bytes 1048576 | tf_op jit(solution)/shard_map/while/body/eval_jaxpr/all_to_all | solution.py:144
  219.0 10.1 %all-to-all-start.2 = ((bf16[8,1,9]{2,1,0:T(2,128)(2,1)}), bf16[8,1,9]{2,1,0:T(2,128)(2,1)S(1)}, u32[]{:S(2)}, u32[]{:S(2)}) async-start(bf16[8,1,9]{2,1,0:T(2,128)(2,1)} %convert_element_type.196), calls=%async_computation.2 | async-start | bytes 8192 | tf_op jit(solution)/shard_map/while/body/eval_jaxpr/all_to_all | solution.py:164
  229.1 15.8 %all-to-all-start.1 = ((bf16[8,9,2048]{2,1,0:T(8,128)(2,1)}), bf16[8,9,2048]{2,1,0:T(8,128)(2,1)S(1)}, u32[]{:S(2)}, u32[]{:S(2)}) async-start(bf16[8,9,2048]{2,1,0:T(8,128)(2,1)} %reshape.306), calls=%async_computation.1 | async-start | bytes 1048576 | tf_op jit(solution)/shard_map/while/body/eval_jaxpr/all_to_all | solution.py:157
  248.1 21.5 %collective-permute-start = (bf16[16,2048]{1,0:T(8,128)(2,1)S(1)}, bf16[16,2048]{1,0:T(8,128)(2,1)S(1)}, u32[]{:S(2)}, u32[]{:S(2)}) collective-permute-start(bf16[16,2048]{1,0:T(8,128)(2,1)S(1)} %broadcast_select_fusion.2), channel_id=1, source_target_pairs={{8,0},{16,8},{24,16},{9,1},{17,9},{25,17},{10,2},{18,10},{26,18},{... | collective-permute-start | bytes 196616 | tf_op jit(solution)/shard_map/while/body/eval_jaxpr/ppermute | solution.py:33
  255.5 11.5 %collective-permute-start.3 = (bf16[1,9,2048]{2,1,0:T(8,128)(2,1)S(1)}, bf16[1,9,2048]{2,1,0:T(8,128)(2,1)S(1)}, u32[]{:S(2)}, u32[]{:S(2)}) collective-permute-start(bf16[1,9,2048]{2,1,0:T(8,128)(2,1)S(1)} %get-tuple-element.647), channel_id=1, source_target_pairs={{0,3},{1,4},{2,5},{3,6},{4,7},{5,0},{6,1},{7,2},{8,11},{9,12},{10,... | collective-permute-start | bytes 110600 | tf_op jit(solution)/shard_map/while/body/eval_jaxpr/ppermute | solution.py:25
  263.2 11.8 %collective-permute-start.6 = (bf16[1,9,2048]{2,1,0:T(8,128)(2,1)S(1)}, bf16[1,9,2048]{2,1,0:T(8,128)(2,1)S(1)}, u32[]{:S(2)}, u32[]{:S(2)}) collective-permute-start(bf16[1,9,2048]{2,1,0:T(8,128)(2,1)S(1)} %get-tuple-element.650), channel_id=1, source_target_pairs={{0,6},{1,7},{2,0},{3,1},{4,2},{5,3},{6,4},{7,5},{8,14},{9,15},{10,... | collective-permute-start | bytes 110600 | tf_op jit(solution)/shard_map/while/body/eval_jaxpr/ppermute | solution.py:25
  271.1 16.6 %all-to-all-start = ((bf16[8,9,2048]{2,1,0:T(8,128)(2,1)}), bf16[8,9,2048]{2,1,0:T(8,128)(2,1)S(1)}, u32[]{:S(2)}, u32[]{:S(2)}) async-start(bf16[8,9,2048]{2,1,0:T(8,128)(2,1)} %reshape.303), calls=%async_computation | async-start | bytes 1048576 | tf_op jit(solution)/shard_map/while/body/eval_jaxpr/all_to_all | solution.py:144
  301.4 10.1 %all-to-all-start.2 = ((bf16[8,1,9]{2,1,0:T(2,128)(2,1)}), bf16[8,1,9]{2,1,0:T(2,128)(2,1)S(1)}, u32[]{:S(2)}, u32[]{:S(2)}) async-start(bf16[8,1,9]{2,1,0:T(2,128)(2,1)} %convert_element_type.196), calls=%async_computation.2 | async-start | bytes 8192 | tf_op jit(solution)/shard_map/while/body/eval_jaxpr/all_to_all | solution.py:164
  311.5 15.8 %all-to-all-start.1 = ((bf16[8,9,2048]{2,1,0:T(8,128)(2,1)}), bf16[8,9,2048]{2,1,0:T(8,128)(2,1)S(1)}, u32[]{:S(2)}, u32[]{:S(2)}) async-start(bf16[8,9,2048]{2,1,0:T(8,128)(2,1)} %reshape.306), calls=%async_computation.1 | async-start | bytes 1048576 | tf_op jit(solution)/shard_map/while/body/eval_jaxpr/all_to_all | solution.py:157
  330.5 21.5 %collective-permute-start = (bf16[16,2048]{1,0:T(8,128)(2,1)S(1)}, bf16[16,2048]{1,0:T(8,128)(2,1)S(1)}, u32[]{:S(2)}, u32[]{:S(2)}) collective-permute-start(bf16[16,2048]{1,0:T(8,128)(2,1)S(1)} %broadcast_select_fusion.2), channel_id=1, source_target_pairs={{8,0},{16,8},{24,16},{9,1},{17,9},{25,17},{10,2},{18,10},{26,18},{... | collective-permute-start | bytes 196616 | tf_op jit(solution)/shard_map/while/body/eval_jaxpr/ppermute | solution.py:33
  337.9 11.5 %collective-permute-start.3 = (bf16[1,9,2048]{2,1,0:T(8,128)(2,1)S(1)}, bf16[1,9,2048]{2,1,0:T(8,128)(2,1)S(1)}, u32[]{:S(2)}, u32[]{:S(2)}) collective-permute-start(bf16[1,9,2048]{2,1,0:T(8,128)(2,1)S(1)} %get-tuple-element.647), channel_id=1, source_target_pairs={{0,3},{1,4},{2,5},{3,6},{4,7},{5,0},{6,1},{7,2},{8,11},{9,12},{10,... | collective-permute-start | bytes 110600 | tf_op jit(solution)/shard_map/while/body/eval_jaxpr/ppermute | solution.py:25
  345.6 11.8 %collective-permute-start.6 = (bf16[1,9,2048]{2,1,0:T(8,128)(2,1)S(1)}, bf16[1,9,2048]{2,1,0:T(8,128)(2,1)S(1)}, u32[]{:S(2)}, u32[]{:S(2)}) collective-permute-start(bf16[1,9,2048]{2,1,0:T(8,128)(2,1)S(1)} %get-tuple-element.650), channel_id=1, source_target_pairs={{0,6},{1,7},{2,0},{3,1},{4,2},{5,3},{6,4},{7,5},{8,14},{9,15},{10,... | collective-permute-start | bytes 110600 | tf_op jit(solution)/shard_map/while/body/eval_jaxpr/ppermute | solution.py:25
  353.5 16.6 %all-to-all-start = ((bf16[8,9,2048]{2,1,0:T(8,128)(2,1)}), bf16[8,9,2048]{2,1,0:T(8,128)(2,1)S(1)}, u32[]{:S(2)}, u32[]{:S(2)}) async-start(bf16[8,9,2048]{2,1,0:T(8,128)(2,1)} %reshape.303), calls=%async_computation | async-start | bytes 1048576 | tf_op jit(solution)/shard_map/while/body/eval_jaxpr/all_to_all | solution.py:144
  383.8 10.1 %all-to-all-start.2 = ((bf16[8,1,9]{2,1,0:T(2,128)(2,1)}), bf16[8,1,9]{2,1,0:T(2,128)(2,1)S(1)}, u32[]{:S(2)}, u32[]{:S(2)}) async-start(bf16[8,1,9]{2,1,0:T(2,128)(2,1)} %convert_element_type.196), calls=%async_computation.2 | async-start | bytes 8192 | tf_op jit(solution)/shard_map/while/body/eval_jaxpr/all_to_all | solution.py:164
  393.9 15.8 %all-to-all-start.1 = ((bf16[8,9,2048]{2,1,0:T(8,128)(2,1)}), bf16[8,9,2048]{2,1,0:T(8,128)(2,1)S(1)}, u32[]{:S(2)}, u32[]{:S(2)}) async-start(bf16[8,9,2048]{2,1,0:T(8,128)(2,1)} %reshape.306), calls=%async_computation.1 | async-start | bytes 1048576 | tf_op jit(solution)/shard_map/while/body/eval_jaxpr/all_to_all | solution.py:157
  412.9 21.5 %collective-permute-start = (bf16[16,2048]{1,0:T(8,128)(2,1)S(1)}, bf16[16,2048]{1,0:T(8,128)(2,1)S(1)}, u32[]{:S(2)}, u32[]{:S(2)}) collective-permute-start(bf16[16,2048]{1,0:T(8,128)(2,1)S(1)} %broadcast_select_fusion.2), channel_id=1, source_target_pairs={{8,0},{16,8},{24,16},{9,1},{17,9},{25,17},{10,2},{18,10},{26,18},{... | collective-permute-start | bytes 196616 | tf_op jit(solution)/shard_map/while/body/eval_jaxpr/ppermute | solution.py:33
  420.3 11.5 %collective-permute-start.3 = (bf16[1,9,2048]{2,1,0:T(8,128)(2,1)S(1)}, bf16[1,9,2048]{2,1,0:T(8,128)(2,1)S(1)}, u32[]{:S(2)}, u32[]{:S(2)}) collective-permute-start(bf16[1,9,2048]{2,1,0:T(8,128)(2,1)S(1)} %get-tuple-element.647), channel_id=1, source_target_pairs={{0,3},{1,4},{2,5},{3,6},{4,7},{5,0},{6,1},{7,2},{8,11},{9,12},{10,... | collective-permute-start | bytes 110600 | tf_op jit(solution)/shard_map/while/body/eval_jaxpr/ppermute | solution.py:25
  428.0 11.8 %collective-permute-start.6 = (bf16[1,9,2048]{2,1,0:T(8,128)(2,1)S(1)}, bf16[1,9,2048]{2,1,0:T(8,128)(2,1)S(1)}, u32[]{:S(2)}, u32[]{:S(2)}) collective-permute-start(bf16[1,9,2048]{2,1,0:T(8,128)(2,1)S(1)} %get-tuple-element.650), channel_id=1, source_target_pairs={{0,6},{1,7},{2,0},{3,1},{4,2},{5,3},{6,4},{7,5},{8,14},{9,15},{10,... | collective-permute-start | bytes 110600 | tf_op jit(solution)/shard_map/while/body/eval_jaxpr/ppermute | solution.py:25
  435.9 16.6 %all-to-all-start = ((bf16[8,9,2048]{2,1,0:T(8,128)(2,1)}), bf16[8,9,2048]{2,1,0:T(8,128)(2,1)S(1)}, u32[]{:S(2)}, u32[]{:S(2)}) async-start(bf16[8,9,2048]{2,1,0:T(8,128)(2,1)} %reshape.303), calls=%async_computation | async-start | bytes 1048576 | tf_op jit(solution)/shard_map/while/body/eval_jaxpr/all_to_all | solution.py:144
  466.2 10.1 %all-to-all-start.2 = ((bf16[8,1,9]{2,1,0:T(2,128)(2,1)}), bf16[8,1,9]{2,1,0:T(2,128)(2,1)S(1)}, u32[]{:S(2)}, u32[]{:S(2)}) async-start(bf16[8,1,9]{2,1,0:T(2,128)(2,1)} %convert_element_type.196), calls=%async_computation.2 | async-start | bytes 8192 | tf_op jit(solution)/shard_map/while/body/eval_jaxpr/all_to_all | solution.py:164
  476.3 15.8 %all-to-all-start.1 = ((bf16[8,9,2048]{2,1,0:T(8,128)(2,1)}), bf16[8,9,2048]{2,1,0:T(8,128)(2,1)S(1)}, u32[]{:S(2)}, u32[]{:S(2)}) async-start(bf16[8,9,2048]{2,1,0:T(8,128)(2,1)} %reshape.306), calls=%async_computation.1 | async-start | bytes 1048576 | tf_op jit(solution)/shard_map/while/body/eval_jaxpr/all_to_all | solution.py:157
  495.3 21.5 %collective-permute-start = (bf16[16,2048]{1,0:T(8,128)(2,1)S(1)}, bf16[16,2048]{1,0:T(8,128)(2,1)S(1)}, u32[]{:S(2)}, u32[]{:S(2)}) collective-permute-start(bf16[16,2048]{1,0:T(8,128)(2,1)S(1)} %broadcast_select_fusion.2), channel_id=1, source_target_pairs={{8,0},{16,8},{24,16},{9,1},{17,9},{25,17},{10,2},{18,10},{26,18},{... | collective-permute-start | bytes 196616 | tf_op jit(solution)/shard_map/while/body/eval_jaxpr/ppermute | solution.py:33
  502.7 11.5 %collective-permute-start.3 = (bf16[1,9,2048]{2,1,0:T(8,128)(2,1)S(1)}, bf16[1,9,2048]{2,1,0:T(8,128)(2,1)S(1)}, u32[]{:S(2)}, u32[]{:S(2)}) collective-permute-start(bf16[1,9,2048]{2,1,0:T(8,128)(2,1)S(1)} %get-tuple-element.647), channel_id=1, source_target_pairs={{0,3},{1,4},{2,5},{3,6},{4,7},{5,0},{6,1},{7,2},{8,11},{9,12},{10,... | collective-permute-start | bytes 110600 | tf_op jit(solution)/shard_map/while/body/eval_jaxpr/ppermute | solution.py:25
  510.4 11.8 %collective-permute-start.6 = (bf16[1,9,2048]{2,1,0:T(8,128)(2,1)S(1)}, bf16[1,9,2048]{2,1,0:T(8,128)(2,1)S(1)}, u32[]{:S(2)}, u32[]{:S(2)}) collective-permute-start(bf16[1,9,2048]{2,1,0:T(8,128)(2,1)S(1)} %get-tuple-element.650), channel_id=1, source_target_pairs={{0,6},{1,7},{2,0},{3,1},{4,2},{5,3},{6,4},{7,5},{8,14},{9,15},{10,... | collective-permute-start | bytes 110600 | tf_op jit(solution)/shard_map/while/body/eval_jaxpr/ppermute | solution.py:25
  518.3 16.6 %all-to-all-start = ((bf16[8,9,2048]{2,1,0:T(8,128)(2,1)}), bf16[8,9,2048]{2,1,0:T(8,128)(2,1)S(1)}, u32[]{:S(2)}, u32[]{:S(2)}) async-start(bf16[8,9,2048]{2,1,0:T(8,128)(2,1)} %reshape.303), calls=%async_computation | async-start | bytes 1048576 | tf_op jit(solution)/shard_map/while/body/eval_jaxpr/all_to_all | solution.py:144
  548.6 10.1 %all-to-all-start.2 = ((bf16[8,1,9]{2,1,0:T(2,128)(2,1)}), bf16[8,1,9]{2,1,0:T(2,128)(2,1)S(1)}, u32[]{:S(2)}, u32[]{:S(2)}) async-start(bf16[8,1,9]{2,1,0:T(2,128)(2,1)} %convert_element_type.196), calls=%async_computation.2 | async-start | bytes 8192 | tf_op jit(solution)/shard_map/while/body/eval_jaxpr/all_to_all | solution.py:164
  558.7 15.8 %all-to-all-start.1 = ((bf16[8,9,2048]{2,1,0:T(8,128)(2,1)}), bf16[8,9,2048]{2,1,0:T(8,128)(2,1)S(1)}, u32[]{:S(2)}, u32[]{:S(2)}) async-start(bf16[8,9,2048]{2,1,0:T(8,128)(2,1)} %reshape.306), calls=%async_computation.1 | async-start | bytes 1048576 | tf_op jit(solution)/shard_map/while/body/eval_jaxpr/all_to_all | solution.py:157
  577.7 21.5 %collective-permute-start = (bf16[16,2048]{1,0:T(8,128)(2,1)S(1)}, bf16[16,2048]{1,0:T(8,128)(2,1)S(1)}, u32[]{:S(2)}, u32[]{:S(2)}) collective-permute-start(bf16[16,2048]{1,0:T(8,128)(2,1)S(1)} %broadcast_select_fusion.2), channel_id=1, source_target_pairs={{8,0},{16,8},{24,16},{9,1},{17,9},{25,17},{10,2},{18,10},{26,18},{... | collective-permute-start | bytes 196616 | tf_op jit(solution)/shard_map/while/body/eval_jaxpr/ppermute | solution.py:33
  585.1 11.5 %collective-permute-start.3 = (bf16[1,9,2048]{2,1,0:T(8,128)(2,1)S(1)}, bf16[1,9,2048]{2,1,0:T(8,128)(2,1)S(1)}, u32[]{:S(2)}, u32[]{:S(2)}) collective-permute-start(bf16[1,9,2048]{2,1,0:T(8,128)(2,1)S(1)} %get-tuple-element.647), channel_id=1, source_target_pairs={{0,3},{1,4},{2,5},{3,6},{4,7},{5,0},{6,1},{7,2},{8,11},{9,12},{10,... | collective-permute-start | bytes 110600 | tf_op jit(solution)/shard_map/while/body/eval_jaxpr/ppermute | solution.py:25
  592.8 11.8 %collective-permute-start.6 = (bf16[1,9,2048]{2,1,0:T(8,128)(2,1)S(1)}, bf16[1,9,2048]{2,1,0:T(8,128)(2,1)S(1)}, u32[]{:S(2)}, u32[]{:S(2)}) collective-permute-start(bf16[1,9,2048]{2,1,0:T(8,128)(2,1)S(1)} %get-tuple-element.650), channel_id=1, source_target_pairs={{0,6},{1,7},{2,0},{3,1},{4,2},{5,3},{6,4},{7,5},{8,14},{9,15},{10,... | collective-permute-start | bytes 110600 | tf_op jit(solution)/shard_map/while/body/eval_jaxpr/ppermute | solution.py:25
  600.7 16.6 %all-to-all-start = ((bf16[8,9,2048]{2,1,0:T(8,128)(2,1)}), bf16[8,9,2048]{2,1,0:T(8,128)(2,1)S(1)}, u32[]{:S(2)}, u32[]{:S(2)}) async-start(bf16[8,9,2048]{2,1,0:T(8,128)(2,1)} %reshape.303), calls=%async_computation | async-start | bytes 1048576 | tf_op jit(solution)/shard_map/while/body/eval_jaxpr/all_to_all | solution.py:144
  631.0 10.1 %all-to-all-start.2 = ((bf16[8,1,9]{2,1,0:T(2,128)(2,1)}), bf16[8,1,9]{2,1,0:T(2,128)(2,1)S(1)}, u32[]{:S(2)}, u32[]{:S(2)}) async-start(bf16[8,1,9]{2,1,0:T(2,128)(2,1)} %convert_element_type.196), calls=%async_computation.2 | async-start | bytes 8192 | tf_op jit(solution)/shard_map/while/body/eval_jaxpr/all_to_all | solution.py:164
  641.1 15.8 %all-to-all-start.1 = ((bf16[8,9,2048]{2,1,0:T(8,128)(2,1)}), bf16[8,9,2048]{2,1,0:T(8,128)(2,1)S(1)}, u32[]{:S(2)}, u32[]{:S(2)}) async-start(bf16[8,9,2048]{2,1,0:T(8,128)(2,1)} %reshape.306), calls=%async_computation.1 | async-start | bytes 1048576 | tf_op jit(solution)/shard_map/while/body/eval_jaxpr/all_to_all | solution.py:157
  660.1 21.5 %collective-permute-start = (bf16[16,2048]{1,0:T(8,128)(2,1)S(1)}, bf16[16,2048]{1,0:T(8,128)(2,1)S(1)}, u32[]{:S(2)}, u32[]{:S(2)}) collective-permute-start(bf16[16,2048]{1,0:T(8,128)(2,1)S(1)} %broadcast_select_fusion.2), channel_id=1, source_target_pairs={{8,0},{16,8},{24,16},{9,1},{17,9},{25,17},{10,2},{18,10},{26,18},{... | collective-permute-start | bytes 196616 | tf_op jit(solution)/shard_map/while/body/eval_jaxpr/ppermute | solution.py:33
  667.5 11.5 %collective-permute-start.3 = (bf16[1,9,2048]{2,1,0:T(8,128)(2,1)S(1)}, bf16[1,9,2048]{2,1,0:T(8,128)(2,1)S(1)}, u32[]{:S(2)}, u32[]{:S(2)}) collective-permute-start(bf16[1,9,2048]{2,1,0:T(8,128)(2,1)S(1)} %get-tuple-element.647), channel_id=1, source_target_pairs={{0,3},{1,4},{2,5},{3,6},{4,7},{5,0},{6,1},{7,2},{8,11},{9,12},{10,... | collective-permute-start | bytes 110600 | tf_op jit(solution)/shard_map/while/body/eval_jaxpr/ppermute | solution.py:25
  675.2 11.8 %collective-permute-start.6 = (bf16[1,9,2048]{2,1,0:T(8,128)(2,1)S(1)}, bf16[1,9,2048]{2,1,0:T(8,128)(2,1)S(1)}, u32[]{:S(2)}, u32[]{:S(2)}) collective-permute-start(bf16[1,9,2048]{2,1,0:T(8,128)(2,1)S(1)} %get-tuple-element.650), channel_id=1, source_target_pairs={{0,6},{1,7},{2,0},{3,1},{4,2},{5,3},{6,4},{7,5},{8,14},{9,15},{10,... | collective-permute-start | bytes 110600 | tf_op jit(solution)/shard_map/while/body/eval_jaxpr/ppermute | solution.py:25
  683.1 16.6 %all-to-all-start = ((bf16[8,9,2048]{2,1,0:T(8,128)(2,1)}), bf16[8,9,2048]{2,1,0:T(8,128)(2,1)S(1)}, u32[]{:S(2)}, u32[]{:S(2)}) async-start(bf16[8,9,2048]{2,1,0:T(8,128)(2,1)} %reshape.303), calls=%async_computation | async-start | bytes 1048576 | tf_op jit(solution)/shard_map/while/body/eval_jaxpr/all_to_all | solution.py:144
  713.4 10.1 %all-to-all-start.2 = ((bf16[8,1,9]{2,1,0:T(2,128)(2,1)}), bf16[8,1,9]{2,1,0:T(2,128)(2,1)S(1)}, u32[]{:S(2)}, u32[]{:S(2)}) async-start(bf16[8,1,9]{2,1,0:T(2,128)(2,1)} %convert_element_type.196), calls=%async_computation.2 | async-start | bytes 8192 | tf_op jit(solution)/shard_map/while/body/eval_jaxpr/all_to_all | solution.py:164
  723.5 13.7 %all-to-all-start.1 = ((bf16[8,9,2048]{2,1,0:T(8,128)(2,1)}), bf16[8,9,2048]{2,1,0:T(8,128)(2,1)S(1)}, u32[]{:S(2)}, u32[]{:S(2)}) async-start(bf16[8,9,2048]{2,1,0:T(8,128)(2,1)} %reshape.306), calls=%async_computation.1 | async-start | bytes 1048576 | tf_op jit(solution)/shard_map/while/body/eval_jaxpr/all_to_all | solution.py:157
  740.5 21.5 %collective-permute-start = (bf16[16,2048]{1,0:T(8,128)(2,1)S(1)}, bf16[16,2048]{1,0:T(8,128)(2,1)S(1)}, u32[]{:S(2)}, u32[]{:S(2)}) collective-permute-start(bf16[16,2048]{1,0:T(8,128)(2,1)S(1)} %broadcast_select_fusion.2), channel_id=1, source_target_pairs={{8,0},{16,8},{24,16},{9,1},{17,9},{25,17},{10,2},{18,10},{26,18},{... | collective-permute-start | bytes 196616 | tf_op jit(solution)/shard_map/while/body/eval_jaxpr/ppermute | solution.py:33
  748.0 11.3 %collective-permute-start.3 = (bf16[1,9,2048]{2,1,0:T(8,128)(2,1)S(1)}, bf16[1,9,2048]{2,1,0:T(8,128)(2,1)S(1)}, u32[]{:S(2)}, u32[]{:S(2)}) collective-permute-start(bf16[1,9,2048]{2,1,0:T(8,128)(2,1)S(1)} %get-tuple-element.647), channel_id=1, source_target_pairs={{0,3},{1,4},{2,5},{3,6},{4,7},{5,0},{6,1},{7,2},{8,11},{9,12},{10,... | collective-permute-start | bytes 110600 | tf_op jit(solution)/shard_map/while/body/eval_jaxpr/ppermute | solution.py:25
  749.4 10.0 %collective-permute-start.4 = (bf16[1,9,2048]{2,1,0:T(8,128)(2,1)S(1)}, bf16[1,9,2048]{2,1,0:T(8,128)(2,1)S(1)}, u32[]{:S(2)}, u32[]{:S(2)}) collective-permute-start(bf16[1,9,2048]{2,1,0:T(8,128)(2,1)S(1)} %get-tuple-element.648), channel_id=1, source_target_pairs={{0,4},{1,5},{2,6},{3,7},{4,0},{5,1},{6,2},{7,3},{8,12},{9,13},{10,... | collective-permute-start | bytes 110600 | tf_op jit(solution)/shard_map/while/body/eval_jaxpr/ppermute | solution.py:25
  755.6 11.8 %collective-permute-start.6 = (bf16[1,9,2048]{2,1,0:T(8,128)(2,1)S(1)}, bf16[1,9,2048]{2,1,0:T(8,128)(2,1)S(1)}, u32[]{:S(2)}, u32[]{:S(2)}) collective-permute-start(bf16[1,9,2048]{2,1,0:T(8,128)(2,1)S(1)} %get-tuple-element.650), channel_id=1, source_target_pairs={{0,6},{1,7},{2,0},{3,1},{4,2},{5,3},{6,4},{7,5},{8,14},{9,15},{10,... | collective-permute-start | bytes 110600 | tf_op jit(solution)/shard_map/while/body/eval_jaxpr/ppermute | solution.py:25
  763.5 16.6 %all-to-all-start = ((bf16[8,9,2048]{2,1,0:T(8,128)(2,1)}), bf16[8,9,2048]{2,1,0:T(8,128)(2,1)S(1)}, u32[]{:S(2)}, u32[]{:S(2)}) async-start(bf16[8,9,2048]{2,1,0:T(8,128)(2,1)} %reshape.303), calls=%async_computation | async-start | bytes 1048576 | tf_op jit(solution)/shard_map/while/body/eval_jaxpr/all_to_all | solution.py:144
  780.8 10.1 %all-to-all-start.2 = ((bf16[8,1,9]{2,1,0:T(2,128)(2,1)}), bf16[8,1,9]{2,1,0:T(2,128)(2,1)S(1)}, u32[]{:S(2)}, u32[]{:S(2)}) async-start(bf16[8,1,9]{2,1,0:T(2,128)(2,1)} %convert_element_type.196), calls=%async_computation.2 | async-start | bytes 8192 | tf_op jit(solution)/shard_map/while/body/eval_jaxpr/all_to_all | solution.py:164
  790.9 15.8 %all-to-all-start.1 = ((bf16[8,9,2048]{2,1,0:T(8,128)(2,1)}), bf16[8,9,2048]{2,1,0:T(8,128)(2,1)S(1)}, u32[]{:S(2)}, u32[]{:S(2)}) async-start(bf16[8,9,2048]{2,1,0:T(8,128)(2,1)} %reshape.306), calls=%async_computation.1 | async-start | bytes 1048576 | tf_op jit(solution)/shard_map/while/body/eval_jaxpr/all_to_all | solution.py:157
  809.9 21.5 %collective-permute-start = (bf16[16,2048]{1,0:T(8,128)(2,1)S(1)}, bf16[16,2048]{1,0:T(8,128)(2,1)S(1)}, u32[]{:S(2)}, u32[]{:S(2)}) collective-permute-start(bf16[16,2048]{1,0:T(8,128)(2,1)S(1)} %broadcast_select_fusion.2), channel_id=1, source_target_pairs={{8,0},{16,8},{24,16},{9,1},{17,9},{25,17},{10,2},{18,10},{26,18},{... | collective-permute-start | bytes 196616 | tf_op jit(solution)/shard_map/while/body/eval_jaxpr/ppermute | solution.py:33
  817.3 11.5 %collective-permute-start.3 = (bf16[1,9,2048]{2,1,0:T(8,128)(2,1)S(1)}, bf16[1,9,2048]{2,1,0:T(8,128)(2,1)S(1)}, u32[]{:S(2)}, u32[]{:S(2)}) collective-permute-start(bf16[1,9,2048]{2,1,0:T(8,128)(2,1)S(1)} %get-tuple-element.647), channel_id=1, source_target_pairs={{0,3},{1,4},{2,5},{3,6},{4,7},{5,0},{6,1},{7,2},{8,11},{9,12},{10,... | collective-permute-start | bytes 110600 | tf_op jit(solution)/shard_map/while/body/eval_jaxpr/ppermute | solution.py:25
  825.0 11.8 %collective-permute-start.6 = (bf16[1,9,2048]{2,1,0:T(8,128)(2,1)S(1)}, bf16[1,9,2048]{2,1,0:T(8,128)(2,1)S(1)}, u32[]{:S(2)}, u32[]{:S(2)}) collective-permute-start(bf16[1,9,2048]{2,1,0:T(8,128)(2,1)S(1)} %get-tuple-element.650), channel_id=1, source_target_pairs={{0,6},{1,7},{2,0},{3,1},{4,2},{5,3},{6,4},{7,5},{8,14},{9,15},{10,... | collective-permute-start | bytes 110600 | tf_op jit(solution)/shard_map/while/body/eval_jaxpr/ppermute | solution.py:25
  832.9 16.6 %all-to-all-start = ((bf16[8,9,2048]{2,1,0:T(8,128)(2,1)}), bf16[8,9,2048]{2,1,0:T(8,128)(2,1)S(1)}, u32[]{:S(2)}, u32[]{:S(2)}) async-start(bf16[8,9,2048]{2,1,0:T(8,128)(2,1)} %reshape.303), calls=%async_computation | async-start | bytes 1048576 | tf_op jit(solution)/shard_map/while/body/eval_jaxpr/all_to_all | solution.py:144
  850.3 10.1 %all-to-all-start.2 = ((bf16[8,1,9]{2,1,0:T(2,128)(2,1)}), bf16[8,1,9]{2,1,0:T(2,128)(2,1)S(1)}, u32[]{:S(2)}, u32[]{:S(2)}) async-start(bf16[8,1,9]{2,1,0:T(2,128)(2,1)} %convert_element_type.196), calls=%async_computation.2 | async-start | bytes 8192 | tf_op jit(solution)/shard_map/while/body/eval_jaxpr/all_to_all | solution.py:164
  860.4 15.8 %all-to-all-start.1 = ((bf16[8,9,2048]{2,1,0:T(8,128)(2,1)}), bf16[8,9,2048]{2,1,0:T(8,128)(2,1)S(1)}, u32[]{:S(2)}, u32[]{:S(2)}) async-start(bf16[8,9,2048]{2,1,0:T(8,128)(2,1)} %reshape.306), calls=%async_computation.1 | async-start | bytes 1048576 | tf_op jit(solution)/shard_map/while/body/eval_jaxpr/all_to_all | solution.py:157
  (100 other events, 993.1 us)
